TPU v7x, 1024 devices: a whole 4x4x32 slice. The times are simulated.
1024 devices in a mesh: dp: 32 (over y, x, core), expert: 32 (over z).
Axes of the slice: x: 4, y: 4, z: 32, core: 2. Of those that a mesh axis runs over, the one named last changes fastest.
Arguments:
- tokens: bfloat16 [1280, 4096], P('expert'), may hold values from -6 to 6
- cotangent: bfloat16 [1280, 4096], P('expert'), may hold values from -6 to 6
- expert_ids: int32 [1280, 8], P('expert'), may hold values from 0 to 63, all different within a row; in each aligned block of 40 rows (0 to 39, 40 to 79, ...) at most 7 rows name the same one
- gate_probs: bfloat16 [1280, 8], P('expert'), may hold values from 0.019897461 to 0.5
- w_gate: bfloat16 [32, 3072, 4096], P('expert', 'dp'), may hold values from -0.09375 to 0.09375
- w_up: bfloat16 [32, 3072, 4096], P('expert', 'dp'), may hold values from -0.09375 to 0.09375
- w_down: bfloat16 [32, 3072, 4096], P('expert', 'dp'), may hold values from -0.15625 to 0.15625
Outputs:
- d_tokens: bfloat16 [1280, 4096], P('expert', 'dp')
- d_probs: float32 [1280, 8], P('expert')
Inputs may be any that keep to these rules, and one draw needn't show every extreme that they name: `expert_ids`: each row names 8 different experts. The 40 rows of one device (aligned blocks of rows) name no expert more than 7 times, a bound that some block reaches.
All inputs are finite; a program needn't handle non-finite values.
Results may differ from a plain program's by a relative error of at most 0.0061.
Values may be sent and summed in bfloat16 or wider, within the bound.
No kernel may reach another device: no remote copies, remote signals or barrier semaphores. Data moves between devices by JAX's collectives and lax.ppermute only.
A program may use at most 32 MiB of HBM per device.

v0:
```python
import jax
import jax.numpy as jnp
from jax import lax
from jax.sharding import PartitionSpec as P

FF = 1536
TOP = 8


def slot_tables(expert_ids, shard_type, group_size, dest_count, send_rows):
    tok_rows, top_count = expert_ids.shape
    flat_ids = expert_ids.reshape(-1)
    chosen = flat_ids % group_size == shard_type
    target = flat_ids // group_size
    columns = lax.broadcasted_iota(jnp.int32, (flat_ids.shape[0], dest_count), 1)
    matched = jnp.logical_and(chosen[:, None], target[:, None] == columns).astype(jnp.int32)
    ranking = jnp.sum((jnp.cumsum(matched, axis=0) - 1) * matched, axis=1)
    row_index = jnp.where(chosen, target * send_rows + ranking, -1)
    rows_iota = lax.broadcasted_iota(jnp.int32, (dest_count * send_rows, flat_ids.shape[0]), 0)
    placing = (rows_iota == row_index[None, :]).astype(jnp.bfloat16)
    by_token = placing.reshape(dest_count * send_rows, tok_rows, top_count).sum(axis=2)
    return (placing, by_token)


def shards(tokens, cotangent, expert_ids, gate_probs, w_gate, w_up, w_down):
    dest_count = lax.axis_size("expert")
    shard_width = w_gate.shape[1]
    shard_count = FF // shard_width
    group_size = lax.axis_size("dp") // shard_count
    shard_type = lax.axis_index("dp") // shard_count
    tok_rows = tokens.shape[0]
    model_width = tokens.shape[1]
    experts_all = group_size * dest_count
    send_rows = (4 * tok_rows * TOP + 3 * experts_all - 1) // (3 * experts_all)
    placing, by_token = slot_tables(expert_ids, shard_type, group_size, dest_count, send_rows)
    rows_sent = jnp.dot(by_token, tokens, preferred_element_type=jnp.float32).astype(jnp.bfloat16)
    rows_sent = rows_sent.reshape(dest_count, send_rows, model_width)
    probs_sent = jnp.dot(
        placing, gate_probs.reshape(-1), preferred_element_type=jnp.float32
    ).astype(jnp.bfloat16)
    probs_sent = probs_sent.reshape(dest_count, send_rows)
    cot_sent = jnp.dot(by_token, cotangent, preferred_element_type=jnp.float32).astype(jnp.bfloat16)
    cot_sent = cot_sent.reshape(dest_count, send_rows, model_width)
    gate_shard = w_gate[0]
    up_shard = w_up[0]
    down_shard = w_down[0]
    contract_model = (((1,), (1,)), ((), ()))
    rows_in, probs_in = (
        lax.all_to_all(rows_sent, "expert", split_axis=0, concat_axis=0, tiled=True),
        lax.all_to_all(probs_sent, "expert", split_axis=0, concat_axis=0, tiled=True),
    )
    cot_in = lax.all_to_all(cot_sent, "expert", split_axis=0, concat_axis=0, tiled=True)
    rows_tok = rows_in.reshape(-1, model_width)
    pre_gate = lax.dot_general(
        rows_tok, gate_shard, contract_model, preferred_element_type=jnp.float32
    )
    pre_up = lax.dot_general(rows_tok, up_shard, contract_model, preferred_element_type=jnp.float32)
    sigmoid_gate = jax.nn.sigmoid(pre_gate)
    activated = pre_gate * sigmoid_gate
    hidden = (activated * pre_up).astype(jnp.bfloat16)
    outputs = jnp.dot(hidden, down_shard, preferred_element_type=jnp.float32).astype(jnp.bfloat16)
    outputs = lax.optimization_barrier(outputs)
    rows_cot = cot_in.reshape(-1, model_width)
    d_hidden = lax.dot_general(
        rows_cot, down_shard, contract_model, preferred_element_type=jnp.float32
    )
    d_hidden = d_hidden * probs_in.reshape(-1, 1).astype(jnp.float32)
    d_up = (d_hidden * activated).astype(jnp.bfloat16)
    d_gate = (d_hidden * pre_up * sigmoid_gate * (1.0 + pre_gate * (1.0 - sigmoid_gate))).astype(
        jnp.bfloat16
    )
    d_rows = jnp.dot(d_gate, gate_shard, preferred_element_type=jnp.float32) + jnp.dot(
        d_up, up_shard, preferred_element_type=jnp.float32
    )
    d_rows = d_rows.astype(jnp.bfloat16).reshape(dest_count, send_rows, model_width)
    out_back = lax.all_to_all(
        outputs.reshape(dest_count, send_rows, model_width),
        "expert",
        split_axis=0,
        concat_axis=0,
        tiled=True,
    )
    grads_back = lax.all_to_all(d_rows, "expert", split_axis=0, concat_axis=0, tiled=True)
    inner_back = jnp.sum(
        cot_sent.astype(jnp.float32) * out_back.astype(jnp.float32), axis=2
    ).astype(jnp.bfloat16)
    contract_rows = (((0,), (0,)), ((), ()))
    token_terms = lax.dot_general(
        by_token,
        grads_back.reshape(-1, model_width),
        contract_rows,
        preferred_element_type=jnp.float32,
    )
    d_tokens = lax.psum_scatter(token_terms, "dp", scatter_dimension=1, tiled=True).astype(
        jnp.bfloat16
    )
    slot_terms = lax.dot_general(
        placing, inner_back.reshape(-1), contract_rows, preferred_element_type=jnp.float32
    )
    d_probs = lax.psum(slot_terms.reshape(tok_rows, TOP), "dp")
    return (d_tokens, d_probs)


def solution(mesh):
    return jax.shard_map(
        shards,
        mesh=mesh,
        in_specs=(
            P("expert", None),
            P("expert", None),
            P("expert", None),
            P("expert", None),
            P("expert", "dp", None),
            P("expert", "dp", None),
            P("expert", "dp", None),
        ),
        out_specs=(P("expert", "dp"), P("expert", None)),
        check_vma=False,
    )
```

profile of v0, /device:TPU:1, one launch (start us, length us, event | category | flops | bytes accessed | tf_op | source)
XLA Modules:
  0.0 957.2 jit_solution(8041124122206557351)
XLA Ops:
  11.3 29.3 %all-to-all-start.1 = ((bf16[32,1,7]{2,1,0:T(2,128)(2,1)}), bf16[32,1,7]{2,1,0:T(2,128)(2,1)S(1)}, u32[]{:S(2)}, u32[]{:S(2)}) async-start(bf16[32,1,7]{2,1,0:T(2,128)(2,1)} %all_to_all.24), calls=%async_computation.1 | async-start | bytes 32768 | tf_op jit(solution)/shard_map/all_to_all | solution.py:50
  40.9 1.6 convolution_convert_fusion.1
  42.5 1.6 reshape.210
  44.1 17.7 %all-to-all-done.1 = bf16[32,1,7]{2,1,0:T(2,128)(2,1)S(1)} async-done(((bf16[32,1,7]{2,1,0:T(2,128)(2,1)}), bf16[32,1,7]{2,1,0:T(2,128)(2,1)S(1)}, u32[]{:S(2)}, u32[]{:S(2)}) %all-to-all-start.1) | async-done | bytes 480 | tf_op jit(solution)/shard_map/all_to_all | solution.py:50
  61.8 4.0 all-to-all-start.2
  65.8 1.9 convolution_convert_fusion.2
  67.8 2.8 reshape.207
  70.6 187.5 %all-to-all-done.2 = bf16[32,7,4096]{2,1,0:T(8,128)(2,1)S(1)} async-done(((bf16[32,7,4096]{2,1,0:T(8,128)(2,1)}), bf16[32,7,4096]{2,1,0:T(8,128)(2,1)S(1)}, u32[]{:S(2)}, u32[]{:S(2)}) %all-to-all-start.2) | async-done | bytes 1835040 | tf_op jit(solution)/shard_map/all_to_all | solution.py:49
  259.4 10.2 %all-to-all-start = ((bf16[32,7,4096]{2,1,0:T(8,128)(2,1)}), bf16[32,7,4096]{2,1,0:T(8,128)(2,1)}, u32[]{:S(2)}, u32[]{:S(2)}) async-start(bf16[32,7,4096]{2,1,0:T(8,128)(2,1)} %reshape.207), calls=%async_computation | async-start | bytes 4194304 | tf_op jit(solution)/shard_map/all_to_all | solution.py:52
  269.8 1.9 reshape.211
  274.2 193.5 %all-to-all-done = bf16[32,7,4096]{2,1,0:T(8,128)(2,1)} async-done(((bf16[32,7,4096]{2,1,0:T(8,128)(2,1)}), bf16[32,7,4096]{2,1,0:T(8,128)(2,1)}, u32[]{:S(2)}, u32[]{:S(2)}) %all-to-all-start) | async-done | bytes 1835040 | tf_op jit(solution)/shard_map/all_to_all | solution.py:52
  467.6 1.9 reshape.208
  469.5 1.9 convolution_multiply_fusion
  472.8 1.7 reshape.212
  474.5 4.1 all-to-all-start.3
  478.6 3.1 convolution_convert_fusion
  481.7 2.8 reshape.214
  484.5 188.4 %all-to-all-done.3 = bf16[32,7,4096]{2,1,0:T(8,128)(2,1)S(1)} async-done(((bf16[32,7,4096]{2,1,0:T(8,128)(2,1)}), bf16[32,7,4096]{2,1,0:T(8,128)(2,1)S(1)}, u32[]{:S(2)}, u32[]{:S(2)}) %all-to-all-start.3) | async-done | bytes 1835040 | tf_op jit(solution)/shard_map/all_to_all | solution.py:83
  674.2 7.8 all-to-all-start.4
  682.0 2.8 reshape.213
  684.8 2.8 fusion.37
  687.6 188.9 %all-to-all-done.4 = bf16[32,7,4096]{2,1,0:T(8,128)(2,1)S(1)} async-done(((bf16[32,7,4096]{2,1,0:T(8,128)(2,1)}), bf16[32,7,4096]{2,1,0:T(8,128)(2,1)S(1)}, u32[]{:S(2)}, u32[]{:S(2)}) %all-to-all-start.4) | async-done | bytes 1835040 | tf_op jit(solution)/shard_map/all_to_all | solution.py:76
  876.5 2.4 multiply_reduce_fusion
  879.6 69.4 %psum.7 = f32[40,8]{0,1:T(8,128)} all-reduce(f32[40,8]{0,1:T(8,128)S(1)} %bitcast.44), channel_id=1, replica_groups=mesh['dp'=32,'expert'=32] {'dp'}, use_global_device_ids=true, to_apply=%region_6.7 | all-reduce | flops 320 | bytes 2560 | tf_op jit(solution)/shard_map/psum | solution.py:100
  (47 shorter events, 13.1 us)
Async XLA Ops:
  7.2 264.5 %copy-start = (bf16[1,96,4096]{2,1,0:T(8,128)(2,1)S(1)}, bf16[1,96,4096]{2,1,0:T(8,128)(2,1)}, u32[]{:S(2)}) copy-start(bf16[1,96,4096]{2,1,0:T(8,128)(2,1)} %param.11) | copy-start | bytes 2359300
  11.3 50.5 %all-to-all-start.1 = ((bf16[32,1,7]{2,1,0:T(2,128)(2,1)}), bf16[32,1,7]{2,1,0:T(2,128)(2,1)S(1)}, u32[]{:S(2)}, u32[]{:S(2)}) async-start(bf16[32,1,7]{2,1,0:T(2,128)(2,1)} %all_to_all.24), calls=%async_computation.1 | async-start | bytes 32768 | tf_op jit(solution)/shard_map/all_to_all | solution.py:50
  44.1 21.7 %copy-start.6 = (bf16[40,4096]{1,0:T(8,128)(2,1)S(1)}, bf16[40,4096]{1,0:T(8,128)(2,1)}, u32[]{:S(2)}) copy-start(bf16[40,4096]{1,0:T(8,128)(2,1)} %param.8) | copy-start | bytes 983044
  61.8 196.3 %all-to-all-start.2 = ((bf16[32,7,4096]{2,1,0:T(8,128)(2,1)}), bf16[32,7,4096]{2,1,0:T(8,128)(2,1)S(1)}, u32[]{:S(2)}, u32[]{:S(2)}) async-start(bf16[32,7,4096]{2,1,0:T(8,128)(2,1)} %reshape.210), calls=%async_computation.2 | async-start | bytes 4194304 | tf_op jit(solution)/shard_map/all_to_all | solution.py:49
  258.1 1.3 copy-start.1
  259.4 208.2 %all-to-all-start = ((bf16[32,7,4096]{2,1,0:T(8,128)(2,1)}), bf16[32,7,4096]{2,1,0:T(8,128)(2,1)}, u32[]{:S(2)}, u32[]{:S(2)}) async-start(bf16[32,7,4096]{2,1,0:T(8,128)(2,1)} %reshape.207), calls=%async_computation | async-start | bytes 4194304 | tf_op jit(solution)/shard_map/all_to_all | solution.py:52
  271.7 1.1 copy-start.3
  469.5 1.9 copy-start.4
  474.5 4.2 copy-start.5
  474.5 198.4 %all-to-all-start.3 = ((bf16[32,7,4096]{2,1,0:T(8,128)(2,1)}), bf16[32,7,4096]{2,1,0:T(8,128)(2,1)S(1)}, u32[]{:S(2)}, u32[]{:S(2)}) async-start(bf16[32,7,4096]{2,1,0:T(8,128)(2,1)} %reshape.212), calls=%async_computation.3 | async-start | bytes 4194304 | tf_op jit(solution)/shard_map/all_to_all | solution.py:83
  672.9 1.3 copy-start.2
  674.2 202.3 %all-to-all-start.4 = ((bf16[32,7,4096]{2,1,0:T(8,128)(2,1)}), bf16[32,7,4096]{2,1,0:T(8,128)(2,1)S(1)}, u32[]{:S(2)}, u32[]{:S(2)}) async-start(bf16[32,7,4096]{2,1,0:T(8,128)(2,1)} %reshape.214), calls=%async_computation.5 | async-start | bytes 4194304 | tf_op jit(solution)/shard_map/all_to_all | solution.py:76
  682.0 267.0 %reduce-scatter.2.cloned.1.call-start = ((), (), s32[]{:S(2)}) async-start(), calls=%async_computation.6 | async-start | bytes 675840 | tf_op jit(solution)/shard_map/reduce_scatter | solution.py:94
Sparse Core Ops, SparseCore 0:
  688.4 129.7 reduce-scatter.1
where the time goes:
time: 958 us; the launch traced here: 957 us
  waiting for transfers between devices  776 us (81%)
  blocking collectives  69.4 us (7%)
  starting transfers between devices  55.5 us (6%)
  local copies, waits for them, and re-layouts  21.7 us (2%)
  matrix products  15.4 us (2%)
  between operations  14.3 us (1%)
    all_to_all x1, waiting for transfers between devices, shards(): lax.all_to_all(cot_sent, 'expert', split_axis=0, concat_axis=0, tiled=True)  193 us
    all_to_all x1, waiting for transfers between devices, shards(): lax.all_to_all(outputs.reshape(dest_count, send_rows, model_width), 'expe...  189 us
    all_to_all x1, waiting for transfers between devices, shards(): lax.all_to_all(d_rows, 'expert', split_axis=0, concat_axis=0, tiled=True)  188 us
    all_to_all x1, waiting for transfers between devices, shards(): lax.all_to_all(rows_sent, 'expert', split_axis=0, concat_axis=0, tiled=True)  187 us
    psum x1, blocking collectives, shards(): d_probs = lax.psum(slot_terms.reshape(tok_rows, TOP), 'dp')  69.4 us
    all_to_all x1, starting transfers between devices, shards(): lax.all_to_all(probs_sent, 'expert', split_axis=0, concat_axis=0, tiled=T...  29.3 us
  transfers between devices with their start and end apart: 6, of which 5 were waited for; matrix products, arithmetic and copies ran while one was open for 3% of the time, Pallas kernels for 0%

commit v1 on v0

v1 whole, which is shorter than its diff:
```python
import jax
import jax.numpy as jnp
from jax import lax
from jax.sharding import Mesh
from jax.sharding import PartitionSpec as P

FF = 1536
TOP = 8
GROUP = 2
HIGH = lax.Precision.HIGHEST


def slot_tables(expert_ids, shard_type, group_size, dest_count, send_rows):
    tok_rows, top_count = expert_ids.shape
    flat_ids = expert_ids.reshape(-1)
    chosen = flat_ids % group_size == shard_type
    target = flat_ids // group_size
    columns = lax.broadcasted_iota(jnp.int32, (flat_ids.shape[0], dest_count), 1)
    matched = jnp.logical_and(chosen[:, None], target[:, None] == columns).astype(jnp.int32)
    ranking = jnp.sum((jnp.cumsum(matched, axis=0) - 1) * matched, axis=1)
    row_index = jnp.where(chosen, target * send_rows + ranking, -1)
    rows_iota = lax.broadcasted_iota(jnp.int32, (dest_count * send_rows, flat_ids.shape[0]), 0)
    placing = (rows_iota == row_index[None, :]).astype(jnp.bfloat16)
    by_token = placing.reshape(dest_count * send_rows, tok_rows, top_count).sum(axis=2)
    return (placing, by_token)


def shards(tokens, cotangent, expert_ids, gate_probs, w_gate, w_up, w_down):
    dest_count = lax.axis_size("expert")
    shard_width = w_gate.shape[1]
    shard_count = FF // shard_width
    group_size = lax.axis_size("l")
    shard_type = lax.axis_index("l")
    part = lax.axis_index("s")
    tok_rows = tokens.shape[0]
    model_width = tokens.shape[1]
    chunk = model_width // shard_count
    out_width = chunk // group_size
    experts_all = group_size * dest_count
    send_rows = (4 * tok_rows * TOP + 3 * experts_all - 1) // (3 * experts_all)
    slots = dest_count * send_rows
    placing, by_token = slot_tables(expert_ids, shard_type, group_size, dest_count, send_rows)

    tok_chunk = lax.dynamic_slice_in_dim(tokens, part * chunk, chunk, axis=1)
    cot_chunk = lax.dynamic_slice_in_dim(cotangent, part * chunk, chunk, axis=1)
    both_chunk = jnp.concatenate([tok_chunk, cot_chunk], axis=1)
    rows_sent = jnp.dot(by_token, both_chunk, preferred_element_type=jnp.float32).astype(jnp.bfloat16)
    rows_sent = rows_sent.reshape(dest_count, send_rows, 2 * chunk)
    probs_sent = jnp.dot(
        placing, gate_probs.reshape(-1), preferred_element_type=jnp.float32
    ).astype(jnp.bfloat16)
    probs_row = jnp.pad(probs_sent.reshape(dest_count, 1, send_rows), ((0, 0), (0, 0), (0, 2 * chunk - send_rows)))
    payload = jnp.concatenate([rows_sent, probs_row], axis=1)
    recv = lax.all_to_all(payload, "expert", split_axis=0, concat_axis=0, tiled=True)
    probs_in = recv[:, send_rows, :send_rows].reshape(slots).astype(jnp.float32)
    rows_in = recv[:, :send_rows, :].reshape(slots, 2 * chunk)

    gathered = lax.all_gather(rows_in, "s", axis=0, tiled=False)
    tok_parts = gathered[:, :, :chunk]
    cot_parts = gathered[:, :, chunk:]
    rows_tok = tok_parts.transpose(1, 0, 2).reshape(slots, model_width)
    rows_cot = cot_parts.transpose(1, 0, 2).reshape(slots, model_width)
    gate_shard = w_gate[0]
    up_shard = w_up[0]
    down_shard = w_down[0]
    contract_model = (((1,), (1,)), ((), ()))
    pre_gate = lax.dot_general(rows_tok, gate_shard, contract_model, preferred_element_type=jnp.float32)
    pre_up = lax.dot_general(rows_tok, up_shard, contract_model, preferred_element_type=jnp.float32)
    sigmoid_gate = jax.nn.sigmoid(pre_gate)
    activated = pre_gate * sigmoid_gate
    hidden = (activated * pre_up).astype(jnp.bfloat16)
    outputs = jnp.dot(hidden, down_shard, preferred_element_type=jnp.float32).astype(jnp.bfloat16)
    outputs = lax.optimization_barrier(outputs)
    inner = jnp.sum(
        rows_cot.astype(jnp.float32) * outputs.astype(jnp.float32), axis=1
    ).astype(jnp.bfloat16)
    d_hidden = lax.dot_general(rows_cot, down_shard, contract_model, preferred_element_type=jnp.float32)
    d_hidden = d_hidden * probs_in.reshape(-1, 1)
    d_up = (d_hidden * activated).astype(jnp.bfloat16)
    d_gate = (d_hidden * pre_up * sigmoid_gate * (1.0 + pre_gate * (1.0 - sigmoid_gate))).astype(
        jnp.bfloat16
    )
    d_rows = jnp.dot(d_gate, gate_shard, preferred_element_type=jnp.float32) + jnp.dot(
        d_up, up_shard, preferred_element_type=jnp.float32
    )
    d_rows = d_rows.astype(jnp.bfloat16)
    d_split = d_rows.reshape(slots, group_size, shard_count, out_width).transpose(2, 0, 1, 3)
    d_split = d_split.reshape(shard_count, slots, chunk)
    pad_rows = (-(slots + 1)) % 16 + 1
    inner_row = jnp.pad(inner, (0, chunk - slots)).reshape(1, 1, chunk)
    inner_row = jnp.broadcast_to(inner_row, (shard_count, 1, chunk))
    extra = jnp.concatenate(
        [inner_row, jnp.zeros((shard_count, pad_rows - 1, chunk), jnp.bfloat16)], axis=1
    )
    ex_send = jnp.concatenate([d_split, extra], axis=1)
    ex_recv = lax.all_to_all(ex_send, "s", split_axis=0, concat_axis=0, tiled=True)
    summed = jnp.sum(ex_recv.astype(jnp.float32), axis=0)
    grads_chunk = summed[:slots].reshape(dest_count, send_rows, chunk)
    inner_sum = summed[slots, :slots].reshape(dest_count, 1, send_rows)
    inner_sum = jnp.pad(inner_sum, ((0, 0), (0, 0), (0, chunk - send_rows)))
    back_send = jnp.concatenate([grads_chunk, inner_sum], axis=1)
    back = lax.all_to_all(back_send, "expert", split_axis=0, concat_axis=0, tiled=True)

    grads_back = back[:, :send_rows, :].reshape(slots, chunk)
    inner_back = back[:, send_rows, :send_rows].reshape(slots)
    contract_rows = (((0,), (0,)), ((), ()))
    token_terms = lax.dot_general(
        by_token.astype(jnp.float32), grads_back, contract_rows,
        preferred_element_type=jnp.float32, precision=HIGH,
    ).reshape(tok_rows, group_size, out_width)
    slot_terms = lax.dot_general(
        placing.astype(jnp.float32), inner_back, contract_rows,
        preferred_element_type=jnp.float32, precision=HIGH,
    ).reshape(tok_rows, TOP)
    mine = lax.dynamic_index_in_dim(token_terms, shard_type, axis=1, keepdims=False)
    other = lax.dynamic_index_in_dim(token_terms, 1 - shard_type, axis=1, keepdims=False)
    pair_send = jnp.concatenate([other, slot_terms], axis=1)
    pair_recv = lax.ppermute(pair_send, "l", perm=[(0, 1), (1, 0)])
    d_tokens = (mine + pair_recv[:, :out_width]).astype(jnp.bfloat16)
    d_probs = slot_terms + pair_recv[:, out_width:]
    return (d_tokens, d_probs)


def solution(mesh):
    names = mesh.axis_names
    devices = mesh.devices
    if names != ("dp", "expert"):
        devices = devices.transpose([names.index("dp"), names.index("expert")])
    dp_size = devices.shape[0]
    split = Mesh(devices.reshape(GROUP, dp_size // GROUP, devices.shape[1]), ("l", "s", "expert"))
    return jax.shard_map(
        shards,
        mesh=split,
        in_specs=(
            P("expert", None),
            P("expert", None),
            P("expert", None),
            P("expert", None),
            P("expert", ("l", "s"), None),
            P("expert", ("l", "s"), None),
            P("expert", ("l", "s"), None),
        ),
        out_specs=(P("expert", ("l", "s")), P("expert", None)),
        check_vma=False,
    )
```

time: 958 us -> 249 us (0.26)
  waiting for transfers between devices: 776 us -> 80.8 us
  blocking collectives: 69.4 us -> 99.4 us
  starting transfers between devices: 55.5 us -> 26.4 us
    all_to_all x5 -> x1, waiting for transfers between devices: 776 us -> 40.5 us  [shards(): lax.all_to_all(back_send, 'expert', split_axis=0, concat_axis=0, tiled=True)]
    all_to_all x0 -> x2, blocking collectives: none -> 99.4 us  [the longest x1 69.6 us: shards(): lax.all_to_all(payload, 'expert', split_axis=0, concat_axis=0, tiled=True)]
    psum x1 -> x0, blocking collectives: 69.4 us -> none  [shards(): d_probs = lax.psum(slot_terms.reshape(tok_rows, TOP), 'dp')]
    all_gather x0 -> x1, waiting for transfers between devices: none -> 38.4 us  [shards(): gathered = lax.all_gather(rows_in, 's', axis=0, tiled=False)]
    all_to_all x5 -> x1, starting transfers between devices: 55.4 us -> 22 us  [shards(): lax.all_to_all(back_send, 'expert', split_axis=0, concat_axis=0, tiled=True)]
    reshape x7 -> x8, local copies, waits for them, and re-layouts: 15.5 us -> 4.62 us  [the longest x1 2.16 us: shards(): d_split = d_split.reshape(shard_count, slots, chunk)]
  transfers between devices with their start and end apart: 6 -> 3, of which waited for: 5 -> 3; matrix products, arithmetic and copies ran while one was open for 3% -> 0% of each run, Pallas kernels for 0% -> 0%
where the time goes in v1:
time: 249 us; the launch traced here: 246 us
  blocking collectives  99.4 us (40%)
  waiting for transfers between devices  80.8 us (32%)
  starting transfers between devices  26.4 us (11%)
  between operations  14.3 us (6%)
  local copies, waits for them, and re-layouts  13 us (5%)
  matrix products  6.05 us (2%)
  other arithmetic  5.88 us (2%)
    all_to_all x1, blocking collectives, shards(): lax.all_to_all(payload, 'expert', split_axis=0, concat_axis=0, tiled=True)  69.6 us
    all_to_all x1, waiting for transfers between devices, shards(): lax.all_to_all(back_send, 'expert', split_axis=0, concat_axis=0, tiled=True)  40.5 us
    all_gather x1, waiting for transfers between devices, shards(): gathered = lax.all_gather(rows_in, 's', axis=0, tiled=False)  38.4 us
    all_to_all x1, blocking collectives, shards(): lax.all_to_all(ex_send, 's', split_axis=0, concat_axis=0, tiled=True)  29.8 us
    all_to_all x1, starting transfers between devices, shards(): lax.all_to_all(back_send, 'expert', split_axis=0, concat_axis=0, tiled=True)  22 us
    unnamed x11, local copies, waits for them, and re-layouts  5.85 us
  transfers between devices with their start and end apart: 3, of which 3 were waited for; matrix products, arithmetic and copies ran while one was open for 0% of the time, Pallas kernels for 0%

profile of v1, /device:TPU:1, one launch (start us, length us, event | category | flops | bytes accessed | tf_op | source)
XLA Modules:
  0.0 245.9 jit_solution(17835589703961914698)
XLA Ops:
  7.2 0.8 copy.57
  8.2 0.9 reduce-window.6
  9.6 0.8 copy.64
  11.0 0.8 constant_dynamic-slice_fusion
  12.2 69.6 %all_to_all.15 = bf16[32,8,512]{2,1,0:T(8,128)(2,1)S(1)} all-to-all(bf16[32,8,512]{2,1,0:T(8,128)(2,1)S(1)} %fusion.17), channel_id=1, replica_groups=mesh['l'=2,'s'=16,'expert'=32] {'expert'}, dimensions={0} | all-to-all | bytes 524288 | tf_op jit(solution)/shard_map/all_to_all | solution.py:54
  81.8 0.8 all_gather_reshape.3
  82.8 38.4 %all-gather.2.cloned.1.call-done = bf16[16,224,512]{2,1,0:T(8,128)(2,1)} async-done(((bf16[1,224,512]{2,1,0:T(8,128)(2,1)}), bf16[16,224,512]{2,1,0:T(8,128)(2,1)}) %all-gather.2.cloned.1.call-update) | async-done | bytes 3670032 | tf_op jit(solution)/shard_map/all_gather | solution.py:58
  121.3 2.3 slice_bitcast_fusion.1
  124.0 0.9 copy-done.1
  124.9 0.7 fusion.4
  125.7 0.7 fusion.7
  127.1 0.7 convolution_multiply_fusion
  128.4 0.7 fusion.2
  129.0 0.7 fusion.1
  130.1 1.8 copy.86
  131.9 2.2 reshape.206
  134.1 2.2 maximum_maximum_fusion
  136.3 29.8 %all_to_all.16 = bf16[16,240,256]{2,1,0:T(8,128)(2,1)S(1)} all-to-all(bf16[16,240,256]{2,1,0:T(8,128)(2,1)S(1)} %maximum_maximum_fusion), channel_id=1, replica_groups=mesh['l'=2,'s'=16,'expert'=32] {'s'}, dimensions={0} | all-to-all | bytes 3932160 | tf_op jit(solution)/shard_map/all_to_all | solution.py:96
  166.6 0.7 select_maximum_fusion
  167.4 22.0 %all-to-all-start.2 = ((f32[32,8,256]{2,1,0:T(8,128)}), f32[32,8,256]{2,1,0:T(8,128)S(1)}, u32[]{:S(2)}, u32[]{:S(2)}) async-start(f32[32,8,256]{2,1,0:T(8,128)} %select_maximum_fusion), calls=%async_computation.2 | async-start | bytes 524288 | tf_op jit(solution)/shard_map/all_to_all | solution.py:102
  189.3 40.5 %all-to-all-done.2 = f32[32,8,256]{2,1,0:T(8,128)S(1)} async-done(((f32[32,8,256]{2,1,0:T(8,128)}), f32[32,8,256]{2,1,0:T(8,128)S(1)}, u32[]{:S(2)}, u32[]{:S(2)}) %all-to-all-start.2) | async-done | bytes 262176 | tf_op jit(solution)/shard_map/all_to_all | solution.py:102
  230.0 1.3 fusion.15
  231.5 4.3 %collective-permute-start = (f32[40,136]{1,0:T(8,128)S(1)}, f32[40,136]{1,0:T(8,128)S(1)}, u32[]{:S(2)}, u32[]{:S(2)}) collective-permute-start(f32[40,136]{1,0:T(8,128)S(1)} %pad_maximum_fusion), channel_id=1, source_target_pairs={{0,512},{512,0},{1,513},{513,1},{2,514},{514,2},{3,515},{515,3},{4... | collective-permute-start | bytes 65288 | tf_op jit(solution)/shard_map/ppermute | solution.py:118
  235.9 1.9 collective-permute-done
  (52 shorter events, 6.1 us)
Async XLA Ops:
  7.2 119.2 %copy-start = (bf16[1,96,4096]{2,1,0:T(8,128)(2,1)S(1)}, bf16[1,96,4096]{2,1,0:T(8,128)(2,1)}, u32[]{:S(2)}) copy-start(bf16[1,96,4096]{2,1,0:T(8,128)(2,1)} %param.13) | copy-start | bytes 2359300
  7.2 114.1 %all-gather.2.cloned.1.call-start = ((), (), s32[]{:S(2)}) async-start(), calls=%async_computation.3 | async-start | bytes 3899392 | tf_op jit(solution)/shard_map/all_gather | solution.py:58
  123.8 1.1 copy-start.1
  124.0 1.6 copy-start.2
  167.4 62.5 %all-to-all-start.2 = ((f32[32,8,256]{2,1,0:T(8,128)}), f32[32,8,256]{2,1,0:T(8,128)S(1)}, u32[]{:S(2)}, u32[]{:S(2)}) async-start(f32[32,8,256]{2,1,0:T(8,128)} %select_maximum_fusion), calls=%async_computation.2 | async-start | bytes 524288 | tf_op jit(solution)/shard_map/all_to_all | solution.py:102
  231.5 6.3 %collective-permute-start = (f32[40,136]{1,0:T(8,128)S(1)}, f32[40,136]{1,0:T(8,128)S(1)}, u32[]{:S(2)}, u32[]{:S(2)}) collective-permute-start(f32[40,136]{1,0:T(8,128)S(1)} %pad_maximum_fusion), channel_id=1, source_target_pairs={{0,512},{512,0},{1,513},{513,1},{2,514},{514,2},{3,515},{515,3},{4... | collective-permute-start | bytes 65288 | tf_op jit(solution)/shard_map/ppermute | solution.py:118
Sparse Core Ops, SparseCore 0:
  82.7 38.5 all-gather.1

commit v2 on v1

--- a/solution.py
+++ b/solution.py
@@ -96,17 +96,20 @@
     ex_recv = lax.all_to_all(ex_send, "s", split_axis=0, concat_axis=0, tiled=True)
     summed = jnp.sum(ex_recv.astype(jnp.float32), axis=0)
     grads_chunk = summed[:slots].reshape(dest_count, send_rows, chunk)
-    inner_sum = summed[slots, :slots].reshape(dest_count, 1, send_rows)
-    inner_sum = jnp.pad(inner_sum, ((0, 0), (0, 0), (0, chunk - send_rows)))
-    back_send = jnp.concatenate([grads_chunk, inner_sum], axis=1)
+    inner_sum = summed[slots, :slots].reshape(dest_count, send_rows)
+    inner_hi = inner_sum.astype(jnp.bfloat16)
+    inner_lo = (inner_sum - inner_hi.astype(jnp.float32)).astype(jnp.bfloat16)
+    inner_pair = jnp.concatenate([inner_hi, inner_lo], axis=1).reshape(dest_count, 1, 2 * send_rows)
+    inner_pair = jnp.pad(inner_pair, ((0, 0), (0, 0), (0, chunk - 2 * send_rows)))
+    back_send = jnp.concatenate([grads_chunk.astype(jnp.bfloat16), inner_pair], axis=1)
     back = lax.all_to_all(back_send, "expert", split_axis=0, concat_axis=0, tiled=True)
 
     grads_back = back[:, :send_rows, :].reshape(slots, chunk)
-    inner_back = back[:, send_rows, :send_rows].reshape(slots)
+    inner_back = back[:, send_rows, :2 * send_rows].astype(jnp.float32)
+    inner_back = (inner_back[:, :send_rows] + inner_back[:, send_rows:]).reshape(slots)
     contract_rows = (((0,), (0,)), ((), ()))
     token_terms = lax.dot_general(
-        by_token.astype(jnp.float32), grads_back, contract_rows,
-        preferred_element_type=jnp.float32, precision=HIGH,
+        by_token, grads_back, contract_rows, preferred_element_type=jnp.float32
     ).reshape(tok_rows, group_size, out_width)
     slot_terms = lax.dot_general(
         placing.astype(jnp.float32), inner_back, contract_rows,

time: 249 us -> 238 us (0.956)
  waiting for transfers between devices: 80.8 us -> 69.7 us
    all_to_all x1, waiting for transfers between devices: 40.5 us -> 29.3 us  [shards(): lax.all_to_all(back_send, 'expert', split_axis=0, concat_axis=0, tiled=True)]
where the time goes in v2:
time: 238 us; the launch traced here: 235 us
  blocking collectives  99.4 us (42%)
  waiting for transfers between devices  69.7 us (29%)
  starting transfers between devices  26.4 us (11%)
  between operations  14.3 us (6%)
  local copies, waits for them, and re-layouts  13 us (5%)
  other arithmetic  6.02 us (3%)
  matrix products  5.99 us (3%)
    all_to_all x1, blocking collectives, shards(): lax.all_to_all(payload, 'expert', split_axis=0, concat_axis=0, tiled=True)  69.6 us
    all_gather x1, waiting for transfers between devices, shards(): gathered = lax.all_gather(rows_in, 's', axis=0, tiled=False)  38.4 us
    all_to_all x1, blocking collectives, shards(): lax.all_to_all(ex_send, 's', split_axis=0, concat_axis=0, tiled=True)  29.8 us
    all_to_all x1, waiting for transfers between devices, shards(): lax.all_to_all(back_send, 'expert', split_axis=0, concat_axis=0, tiled=True)  29.3 us
    all_to_all x1, starting transfers between devices, shards(): lax.all_to_all(back_send, 'expert', split_axis=0, concat_axis=0, tiled=True)  22 us
    unnamed x11, local copies, waits for them, and re-layouts  5.85 us
  transfers between devices with their start and end apart: 3, of which 3 were waited for; matrix products, arithmetic and copies ran while one was open for 0% of the time, Pallas kernels for 0%

profile of v2, /device:TPU:1, one launch (start us, length us, event | category | flops | bytes accessed | tf_op | source)
XLA Modules:
  0.0 234.8 jit_solution(12927674582580175295)
XLA Ops:
  7.2 0.8 copy.58
  8.2 0.9 reduce-window.6
  9.6 0.8 copy.65
  11.0 0.8 constant_dynamic-slice_fusion
  12.2 69.6 %all_to_all.15 = bf16[32,8,512]{2,1,0:T(8,128)(2,1)S(1)} all-to-all(bf16[32,8,512]{2,1,0:T(8,128)(2,1)S(1)} %fusion.17), channel_id=1, replica_groups=mesh['l'=2,'s'=16,'expert'=32] {'expert'}, dimensions={0} | all-to-all | bytes 524288 | tf_op jit(solution)/shard_map/all_to_all | solution.py:54
  81.8 0.8 all_gather_reshape.3
  82.8 38.4 %all-gather.2.cloned.1.call-done = bf16[16,224,512]{2,1,0:T(8,128)(2,1)} async-done(((bf16[1,224,512]{2,1,0:T(8,128)(2,1)}), bf16[16,224,512]{2,1,0:T(8,128)(2,1)}) %all-gather.2.cloned.1.call-update) | async-done | bytes 3670032 | tf_op jit(solution)/shard_map/all_gather | solution.py:58
  121.3 2.3 slice_bitcast_fusion.1
  124.0 0.9 copy-done.1
  124.9 0.7 fusion.4
  125.7 0.7 fusion.7
  127.1 0.7 convolution_multiply_fusion
  128.4 0.7 fusion.2
  129.0 0.7 fusion.1
  130.1 1.8 copy.90
  131.9 2.2 reshape.213
  134.1 2.2 maximum_maximum_fusion
  136.3 29.8 %all_to_all.16 = bf16[16,240,256]{2,1,0:T(8,128)(2,1)S(1)} all-to-all(bf16[16,240,256]{2,1,0:T(8,128)(2,1)S(1)} %maximum_maximum_fusion), channel_id=1, replica_groups=mesh['l'=2,'s'=16,'expert'=32] {'s'}, dimensions={0} | all-to-all | bytes 3932160 | tf_op jit(solution)/shard_map/all_to_all | solution.py:96
  166.7 0.7 fusion.22
  167.4 22.0 %all-to-all-start.2 = ((bf16[32,8,256]{2,1,0:T(8,128)(2,1)}), bf16[32,8,256]{2,1,0:T(8,128)(2,1)S(1)}, u32[]{:S(2)}, u32[]{:S(2)}) async-start(bf16[32,8,256]{2,1,0:T(8,128)(2,1)} %fusion.22), calls=%async_computation.2 | async-start | bytes 262144 | tf_op jit(solution)/shard_map/all_to_all | solution.py:105
  189.4 29.3 %all-to-all-done.2 = bf16[32,8,256]{2,1,0:T(8,128)(2,1)S(1)} async-done(((bf16[32,8,256]{2,1,0:T(8,128)(2,1)}), bf16[32,8,256]{2,1,0:T(8,128)(2,1)S(1)}, u32[]{:S(2)}, u32[]{:S(2)}) %all-to-all-start.2) | async-done | bytes 131104 | tf_op jit(solution)/shard_map/all_to_all | solution.py:105
  218.9 1.3 fusion.15
  220.4 4.3 %collective-permute-start = (f32[40,136]{1,0:T(8,128)S(1)}, f32[40,136]{1,0:T(8,128)S(1)}, u32[]{:S(2)}, u32[]{:S(2)}) collective-permute-start(f32[40,136]{1,0:T(8,128)S(1)} %pad_maximum_fusion), channel_id=1, source_target_pairs={{0,512},{512,0},{1,513},{513,1},{2,514},{514,2},{3,515},{515,3},{4... | collective-permute-start | bytes 65288 | tf_op jit(solution)/shard_map/ppermute | solution.py:121
  224.8 1.9 collective-permute-done
  (56 shorter events, 6.2 us)
Async XLA Ops:
  7.2 119.2 %copy-start = (bf16[1,96,4096]{2,1,0:T(8,128)(2,1)S(1)}, bf16[1,96,4096]{2,1,0:T(8,128)(2,1)}, u32[]{:S(2)}) copy-start(bf16[1,96,4096]{2,1,0:T(8,128)(2,1)} %param.13) | copy-start | bytes 2359300
  7.2 114.1 %all-gather.2.cloned.1.call-start = ((), (), s32[]{:S(2)}) async-start(), calls=%async_computation.3 | async-start | bytes 3899392 | tf_op jit(solution)/shard_map/all_gather | solution.py:58
  123.8 1.1 copy-start.1
  124.0 1.6 copy-start.2
  167.4 51.3 %all-to-all-start.2 = ((bf16[32,8,256]{2,1,0:T(8,128)(2,1)}), bf16[32,8,256]{2,1,0:T(8,128)(2,1)S(1)}, u32[]{:S(2)}, u32[]{:S(2)}) async-start(bf16[32,8,256]{2,1,0:T(8,128)(2,1)} %fusion.22), calls=%async_computation.2 | async-start | bytes 262144 | tf_op jit(solution)/shard_map/all_to_all | solution.py:105
  220.4 6.3 %collective-permute-start = (f32[40,136]{1,0:T(8,128)S(1)}, f32[40,136]{1,0:T(8,128)S(1)}, u32[]{:S(2)}, u32[]{:S(2)}) collective-permute-start(f32[40,136]{1,0:T(8,128)S(1)} %pad_maximum_fusion), channel_id=1, source_target_pairs={{0,512},{512,0},{1,513},{513,1},{2,514},{514,2},{3,515},{515,3},{4... | collective-permute-start | bytes 65288 | tf_op jit(solution)/shard_map/ppermute | solution.py:121
Sparse Core Ops, SparseCore 0:
  82.7 38.5 all-gather.1

commit v3 on v2

--- a/solution.py
+++ b/solution.py
@@ -25,8 +25,25 @@
     return (placing, by_token)
 
 
+def z_exchange(x):
+    nh = lax.axis_size("zh")
+    nl = lax.axis_size("zl")
+    ih = lax.axis_index("zh")
+    rest = x.shape[1:]
+    x4 = x.reshape((nh, nl) + rest)
+    y = lax.dynamic_slice_in_dim(jnp.concatenate([x4, x4], axis=0), ih, nh, axis=0)
+    parts = [y[0]]
+    for d in range(1, nh):
+        parts.append(lax.ppermute(y[d], "zh", perm=[(h, (h + d) % nh) for h in range(nh)]))
+    z = jnp.stack(parts, axis=1)
+    w = lax.all_to_all(z, "zl", split_axis=0, concat_axis=0, tiled=True)
+    w_rev = w[:, ::-1]
+    v = lax.dynamic_slice_in_dim(jnp.concatenate([w_rev, w_rev], axis=1), (nh - 1 - ih) % nh, nh, axis=1)
+    return jnp.swapaxes(v, 0, 1).reshape((nh * nl,) + rest)
+
+
 def shards(tokens, cotangent, expert_ids, gate_probs, w_gate, w_up, w_down):
-    dest_count = lax.axis_size("expert")
+    dest_count = lax.axis_size("zh") * lax.axis_size("zl")
     shard_width = w_gate.shape[1]
     shard_count = FF // shard_width
     group_size = lax.axis_size("l")
@@ -51,7 +68,7 @@
     ).astype(jnp.bfloat16)
     probs_row = jnp.pad(probs_sent.reshape(dest_count, 1, send_rows), ((0, 0), (0, 0), (0, 2 * chunk - send_rows)))
     payload = jnp.concatenate([rows_sent, probs_row], axis=1)
-    recv = lax.all_to_all(payload, "expert", split_axis=0, concat_axis=0, tiled=True)
+    recv = z_exchange(payload)
     probs_in = recv[:, send_rows, :send_rows].reshape(slots).astype(jnp.float32)
     rows_in = recv[:, :send_rows, :].reshape(slots, 2 * chunk)
 
@@ -102,7 +119,7 @@
     inner_pair = jnp.concatenate([inner_hi, inner_lo], axis=1).reshape(dest_count, 1, 2 * send_rows)
     inner_pair = jnp.pad(inner_pair, ((0, 0), (0, 0), (0, chunk - 2 * send_rows)))
     back_send = jnp.concatenate([grads_chunk.astype(jnp.bfloat16), inner_pair], axis=1)
-    back = lax.all_to_all(back_send, "expert", split_axis=0, concat_axis=0, tiled=True)
+    back = z_exchange(back_send)
 
     grads_back = back[:, :send_rows, :].reshape(slots, chunk)
     inner_back = back[:, send_rows, :2 * send_rows].astype(jnp.float32)
@@ -130,19 +147,23 @@
     if names != ("dp", "expert"):
         devices = devices.transpose([names.index("dp"), names.index("expert")])
     dp_size = devices.shape[0]
-    split = Mesh(devices.reshape(GROUP, dp_size // GROUP, devices.shape[1]), ("l", "s", "expert"))
+    z_size = devices.shape[1]
+    z_low = 8 if z_size % 8 == 0 else z_size
+    split = Mesh(
+        devices.reshape(GROUP, dp_size // GROUP, z_size // z_low, z_low), ("l", "s", "zh", "zl")
+    )
     return jax.shard_map(
         shards,
         mesh=split,
         in_specs=(
-            P("expert", None),
-            P("expert", None),
-            P("expert", None),
-            P("expert", None),
-            P("expert", ("l", "s"), None),
-            P("expert", ("l", "s"), None),
-            P("expert", ("l", "s"), None),
+            P(("zh", "zl"), None),
+            P(("zh", "zl"), None),
+            P(("zh", "zl"), None),
+            P(("zh", "zl"), None),
+            P(("zh", "zl"), ("l", "s"), None),
+            P(("zh", "zl"), ("l", "s"), None),
+            P(("zh", "zl"), ("l", "s"), None),
         ),
-        out_specs=(P("expert", ("l", "s")), P("expert", None)),
+        out_specs=(P(("zh", "zl"), ("l", "s")), P(("zh", "zl"), None)),
         check_vma=False,
     )

time: 238 us -> 259 us (1.088)
  blocking collectives: 99.4 us -> 29.8 us
  starting transfers between devices: 26.4 us -> 93.8 us
  waiting for transfers between devices: 69.7 us -> 90.8 us
    ppermute x0 -> x6, starting transfers between devices: none -> 79.7 us  [z_exchange(): lax.ppermute(y[d], 'zh', perm=[(h, (h + d) % nh) for h in range(nh)])]
    all_to_all x1 -> x0, blocking collectives: 69.6 us -> none  [shards(): lax.all_to_all(payload, 'expert', split_axis=0, concat_axis=0, tiled=True)]
    ppermute x0 -> x6, waiting for transfers between devices: none -> 17.2 us  [z_exchange(): lax.ppermute(y[d], 'zh', perm=[(h, (h + d) % nh) for h in range(nh)])]
    all_to_all x1 -> x2, starting transfers between devices: 22 us -> 9.66 us  [z_exchange(): w = lax.all_to_all(z, 'zl', split_axis=0, concat_axis=0, tiled=True)]
    all_gather x1, waiting for transfers between devices: 38.4 us -> 49.5 us  [shards(): gathered = lax.all_gather(rows_in, 's', axis=0, tiled=False)]
    all_to_all x1 -> x2, waiting for transfers between devices: 29.3 us -> 22.2 us  [z_exchange(): w = lax.all_to_all(z, 'zl', split_axis=0, concat_axis=0, tiled=True)]
  transfers between devices with their start and end apart: 3 -> 10, of which waited for: 3 -> 7; matrix products, arithmetic and copies ran while one was open for 0% -> 0% of each run, Pallas kernels for 0% -> 0%
where the time goes in v3:
time: 259 us; the launch traced here: 255 us
  starting transfers between devices  93.8 us (36%)
  waiting for transfers between devices  90.8 us (35%)
  blocking collectives  29.8 us (12%)
  between operations  14.5 us (6%)
  local copies, waits for them, and re-layouts  13.8 us (5%)
  other arithmetic  6.58 us (3%)
  matrix products  5.99 us (2%)
    ppermute x6, starting transfers between devices, z_exchange(): lax.ppermute(y[d], 'zh', perm=[(h, (h + d) % nh) for h in range(nh)])  79.7 us
    all_gather x1, waiting for transfers between devices, shards(): gathered = lax.all_gather(rows_in, 's', axis=0, tiled=False)  49.5 us
    all_to_all x1, blocking collectives, shards(): lax.all_to_all(ex_send, 's', split_axis=0, concat_axis=0, tiled=True)  29.8 us
    all_to_all x2, waiting for transfers between devices, z_exchange(): w = lax.all_to_all(z, 'zl', split_axis=0, concat_axis=0, tiled=True)  22.2 us
    ppermute x6, waiting for transfers between devices, z_exchange(): lax.ppermute(y[d], 'zh', perm=[(h, (h + d) % nh) for h in range(nh)])  17.2 us
    all_to_all x2, starting transfers between devices, z_exchange(): w = lax.all_to_all(z, 'zl', split_axis=0, concat_axis=0, tiled=True)  9.66 us
    unnamed x11, local copies, waits for them, and re-layouts  5.85 us
  transfers between devices with their start and end apart: 10, of which 7 were waited for; matrix products, arithmetic and copies ran while one was open for 0% of the time, Pallas kernels for 0%

profile of v3, /device:TPU:1, one launch (start us, length us, event | category | flops | bytes accessed | tf_op | source)
XLA Modules:
  0.0 255.4 jit_solution(5949712009364613387)
XLA Ops:
  8.2 0.9 reduce-window.6
  12.5 29.5 %collective-permute-start.1 = (bf16[8,8,512]{2,1,0:T(8,128)(2,1)S(1)}, bf16[8,8,512]{2,1,0:T(8,128)(2,1)S(1)}, u32[]{:S(2)}, u32[]{:S(2)}) collective-permute-start(bf16[8,8,512]{2,1,0:T(8,128)(2,1)S(1)} %get-tuple-element.19), channel_id=1, source_target_pairs={{0,16},{8,24},{16,0},{24,8},{1,17},{9,25},{17,1},{25,9},{2,18},{10... | collective-permute-start | bytes 196616 | tf_op jit(solution)/shard_map/ppermute | solution.py:37
  42.0 5.8 %collective-permute-start = (bf16[8,8,512]{2,1,0:T(8,128)(2,1)S(1)}, bf16[8,8,512]{2,1,0:T(8,128)(2,1)S(1)}, u32[]{:S(2)}, u32[]{:S(2)}) collective-permute-start(bf16[8,8,512]{2,1,0:T(8,128)(2,1)S(1)} %get-tuple-element.20), channel_id=1, source_target_pairs={{0,8},{8,16},{16,24},{24,0},{1,9},{9,17},{17,25},{25,1},{2,10},{10... | collective-permute-start | bytes 196616 | tf_op jit(solution)/shard_map/ppermute | solution.py:37
  47.9 8.2 %collective-permute-start.2 = (bf16[8,8,512]{2,1,0:T(8,128)(2,1)S(1)}, bf16[8,8,512]{2,1,0:T(8,128)(2,1)S(1)}, u32[]{:S(2)}, u32[]{:S(2)}) collective-permute-start(bf16[8,8,512]{2,1,0:T(8,128)(2,1)S(1)} %get-tuple-element.21), channel_id=1, source_target_pairs={{0,24},{8,0},{16,8},{24,16},{1,25},{9,1},{17,9},{25,17},{2,26},{10... | collective-permute-start | bytes 196616 | tf_op jit(solution)/shard_map/ppermute | solution.py:37
  56.1 2.9 %collective-permute-done = bf16[8,8,512]{2,1,0:T(8,128)(2,1)S(1)} collective-permute-done((bf16[8,8,512]{2,1,0:T(8,128)(2,1)S(1)}, bf16[8,8,512]{2,1,0:T(8,128)(2,1)S(1)}, u32[]{:S(2)}, u32[]{:S(2)}) %collective-permute-start) | collective-permute-done | bytes 65568 | tf_op jit(solution)/shard_map/ppermute | solution.py:37
  59.0 9.9 %collective-permute-done.2 = bf16[8,8,512]{2,1,0:T(8,128)(2,1)S(1)} collective-permute-done((bf16[8,8,512]{2,1,0:T(8,128)(2,1)S(1)}, bf16[8,8,512]{2,1,0:T(8,128)(2,1)S(1)}, u32[]{:S(2)}, u32[]{:S(2)}) %collective-permute-start.2) | collective-permute-done | bytes 65568 | tf_op jit(solution)/shard_map/ppermute | solution.py:37
  69.7 5.0 %all-to-all-start = ((bf16[8,4,8,512]{3,2,1,0:T(8,128)(2,1)}), bf16[8,4,8,512]{3,2,1,0:T(8,128)(2,1)S(1)}, u32[]{:S(2)}, u32[]{:S(2)}) async-start(bf16[8,4,8,512]{3,2,1,0:T(8,128)(2,1)} %copy.100), calls=%async_computation | async-start | bytes 524288 | tf_op jit(solution)/shard_map/all_to_all | solution.py:39
  74.8 11.9 %all-to-all-done = bf16[8,4,8,512]{3,2,1,0:T(8,128)(2,1)S(1)} async-done(((bf16[8,4,8,512]{3,2,1,0:T(8,128)(2,1)}), bf16[8,4,8,512]{3,2,1,0:T(8,128)(2,1)S(1)}, u32[]{:S(2)}, u32[]{:S(2)}) %all-to-all-start) | async-done | bytes 262176 | tf_op jit(solution)/shard_map/all_to_all | solution.py:39
  87.9 49.5 %all-gather.2.cloned.1.call-done = bf16[16,224,512]{2,1,0:T(8,128)(2,1)} async-done(((bf16[1,224,512]{2,1,0:T(8,128)(2,1)}), bf16[16,224,512]{2,1,0:T(8,128)(2,1)}) %all-gather.2.cloned.1.call-update) | async-done | bytes 3670032 | tf_op jit(solution)/shard_map/all_gather | solution.py:75
  137.4 2.3 slice_bitcast_fusion.1
  140.2 0.9 copy-done.1
  146.3 1.8 copy.129
  148.0 2.2 reshape.224
  150.2 2.2 maximum_maximum_fusion
  152.4 29.8 %all_to_all.15 = bf16[16,240,256]{2,1,0:T(8,128)(2,1)S(1)} all-to-all(bf16[16,240,256]{2,1,0:T(8,128)(2,1)S(1)} %maximum_maximum_fusion), channel_id=1, replica_groups=mesh['l'=2,'s'=16,'zh'=4,'zl'=8] {'s'}, dimensions={0} | all-to-all | bytes 3932160 | tf_op jit(solution)/shard_map/all_to_all | solution.py:113
  183.1 22.2 %collective-permute-start.4 = (bf16[8,8,256]{2,1,0:T(8,128)(2,1)S(1)}, bf16[8,8,256]{2,1,0:T(8,128)(2,1)S(1)}, u32[]{:S(2)}, u32[]{:S(2)}) collective-permute-start(bf16[8,8,256]{2,1,0:T(8,128)(2,1)S(1)} %get-tuple-element.23), channel_id=1, source_target_pairs={{0,16},{8,24},{16,0},{24,8},{1,17},{9,25},{17,1},{25,9},{2,18},{10... | collective-permute-start | bytes 98312 | tf_op jit(solution)/shard_map/ppermute | solution.py:37
  205.3 2.9 %collective-permute-start.3 = (bf16[8,8,256]{2,1,0:T(8,128)(2,1)S(1)}, bf16[8,8,256]{2,1,0:T(8,128)(2,1)S(1)}, u32[]{:S(2)}, u32[]{:S(2)}) collective-permute-start(bf16[8,8,256]{2,1,0:T(8,128)(2,1)S(1)} %get-tuple-element.24), channel_id=1, source_target_pairs={{0,8},{8,16},{16,24},{24,0},{1,9},{9,17},{17,25},{25,1},{2,10},{10... | collective-permute-start | bytes 98312 | tf_op jit(solution)/shard_map/ppermute | solution.py:37
  208.2 11.1 %collective-permute-start.5 = (bf16[8,8,256]{2,1,0:T(8,128)(2,1)S(1)}, bf16[8,8,256]{2,1,0:T(8,128)(2,1)S(1)}, u32[]{:S(2)}, u32[]{:S(2)}) collective-permute-start(bf16[8,8,256]{2,1,0:T(8,128)(2,1)S(1)} %get-tuple-element.25), channel_id=1, source_target_pairs={{0,24},{8,0},{16,8},{24,16},{1,25},{9,1},{17,9},{25,17},{2,26},{10... | collective-permute-start | bytes 98312 | tf_op jit(solution)/shard_map/ppermute | solution.py:37
  219.3 4.3 %collective-permute-done.5 = bf16[8,8,256]{2,1,0:T(8,128)(2,1)S(1)} collective-permute-done((bf16[8,8,256]{2,1,0:T(8,128)(2,1)S(1)}, bf16[8,8,256]{2,1,0:T(8,128)(2,1)S(1)}, u32[]{:S(2)}, u32[]{:S(2)}) %collective-permute-start.5) | collective-permute-done | bytes 32800 | tf_op jit(solution)/shard_map/ppermute | solution.py:37
  224.3 4.6 %all-to-all-start.2 = ((bf16[8,4,8,256]{3,2,1,0:T(8,128)(2,1)}), bf16[8,4,8,256]{3,2,1,0:T(8,128)(2,1)S(1)}, u32[]{:S(2)}, u32[]{:S(2)}) async-start(bf16[8,4,8,256]{3,2,1,0:T(8,128)(2,1)} %pad_maximum_fusion.1), calls=%async_computation.2 | async-start | bytes 262144 | tf_op jit(solution)/shard_map/all_to_all | solution.py:39
  228.9 10.3 %all-to-all-done.2 = bf16[8,4,8,256]{3,2,1,0:T(8,128)(2,1)S(1)} async-done(((bf16[8,4,8,256]{3,2,1,0:T(8,128)(2,1)}), bf16[8,4,8,256]{3,2,1,0:T(8,128)(2,1)S(1)}, u32[]{:S(2)}, u32[]{:S(2)}) %all-to-all-start.2) | async-done | bytes 131104 | tf_op jit(solution)/shard_map/all_to_all | solution.py:39
  239.5 1.3 fusion.14
  241.0 4.3 %collective-permute-start.6 = (f32[40,136]{1,0:T(8,128)S(1)}, f32[40,136]{1,0:T(8,128)S(1)}, u32[]{:S(2)}, u32[]{:S(2)}) collective-permute-start(f32[40,136]{1,0:T(8,128)S(1)} %pad_maximum_fusion.2), channel_id=1, source_target_pairs={{0,512},{512,0},{1,513},{513,1},{2,514},{514,2},{3,515},{515,3},{4... | collective-permute-start | bytes 65288 | tf_op jit(solution)/shard_map/ppermute | solution.py:138
  245.3 1.9 collective-permute-done.6
  (83 shorter events, 15.0 us)
Async XLA Ops:
  7.2 135.4 %copy-start = (bf16[1,96,4096]{2,1,0:T(8,128)(2,1)S(1)}, bf16[1,96,4096]{2,1,0:T(8,128)(2,1)}, u32[]{:S(2)}) copy-start(bf16[1,96,4096]{2,1,0:T(8,128)(2,1)} %param.13) | copy-start | bytes 2359300
  12.5 43.5 %collective-permute-start.1 = (bf16[8,8,512]{2,1,0:T(8,128)(2,1)S(1)}, bf16[8,8,512]{2,1,0:T(8,128)(2,1)S(1)}, u32[]{:S(2)}, u32[]{:S(2)}) collective-permute-start(bf16[8,8,512]{2,1,0:T(8,128)(2,1)S(1)} %get-tuple-element.19), channel_id=1, source_target_pairs={{0,16},{8,24},{16,0},{24,8},{1,17},{9,25},{17,1},{25,9},{2,18},{10... | collective-permute-start | bytes 196616 | tf_op jit(solution)/shard_map/ppermute | solution.py:37
  42.0 17.0 %collective-permute-start = (bf16[8,8,512]{2,1,0:T(8,128)(2,1)S(1)}, bf16[8,8,512]{2,1,0:T(8,128)(2,1)S(1)}, u32[]{:S(2)}, u32[]{:S(2)}) collective-permute-start(bf16[8,8,512]{2,1,0:T(8,128)(2,1)S(1)} %get-tuple-element.20), channel_id=1, source_target_pairs={{0,8},{8,16},{16,24},{24,0},{1,9},{9,17},{17,25},{25,1},{2,10},{10... | collective-permute-start | bytes 196616 | tf_op jit(solution)/shard_map/ppermute | solution.py:37
  47.9 21.1 %collective-permute-start.2 = (bf16[8,8,512]{2,1,0:T(8,128)(2,1)S(1)}, bf16[8,8,512]{2,1,0:T(8,128)(2,1)S(1)}, u32[]{:S(2)}, u32[]{:S(2)}) collective-permute-start(bf16[8,8,512]{2,1,0:T(8,128)(2,1)S(1)} %get-tuple-element.21), channel_id=1, source_target_pairs={{0,24},{8,0},{16,8},{24,16},{1,25},{9,1},{17,9},{25,17},{2,26},{10... | collective-permute-start | bytes 196616 | tf_op jit(solution)/shard_map/ppermute | solution.py:37
  69.7 17.0 %all-to-all-start = ((bf16[8,4,8,512]{3,2,1,0:T(8,128)(2,1)}), bf16[8,4,8,512]{3,2,1,0:T(8,128)(2,1)S(1)}, u32[]{:S(2)}, u32[]{:S(2)}) async-start(bf16[8,4,8,512]{3,2,1,0:T(8,128)(2,1)} %copy.100), calls=%async_computation | async-start | bytes 524288 | tf_op jit(solution)/shard_map/all_to_all | solution.py:39
  74.7 62.7 %all-gather.2.cloned.1.call-start = ((), (), s32[]{:S(2)}) async-start(), calls=%async_computation.3 | async-start | bytes 3899392 | tf_op jit(solution)/shard_map/all_gather | solution.py:75
  139.9 1.1 copy-start.1
  140.2 1.6 copy-start.2
  183.1 36.3 %collective-permute-start.4 = (bf16[8,8,256]{2,1,0:T(8,128)(2,1)S(1)}, bf16[8,8,256]{2,1,0:T(8,128)(2,1)S(1)}, u32[]{:S(2)}, u32[]{:S(2)}) collective-permute-start(bf16[8,8,256]{2,1,0:T(8,128)(2,1)S(1)} %get-tuple-element.23), channel_id=1, source_target_pairs={{0,16},{8,24},{16,0},{24,8},{1,17},{9,25},{17,1},{25,9},{2,18},{10... | collective-permute-start | bytes 98312 | tf_op jit(solution)/shard_map/ppermute | solution.py:37
  205.3 14.0 %collective-permute-start.3 = (bf16[8,8,256]{2,1,0:T(8,128)(2,1)S(1)}, bf16[8,8,256]{2,1,0:T(8,128)(2,1)S(1)}, u32[]{:S(2)}, u32[]{:S(2)}) collective-permute-start(bf16[8,8,256]{2,1,0:T(8,128)(2,1)S(1)} %get-tuple-element.24), channel_id=1, source_target_pairs={{0,8},{8,16},{16,24},{24,0},{1,9},{9,17},{17,25},{25,1},{2,10},{10... | collective-permute-start | bytes 98312 | tf_op jit(solution)/shard_map/ppermute | solution.py:37
  208.2 15.4 %collective-permute-start.5 = (bf16[8,8,256]{2,1,0:T(8,128)(2,1)S(1)}, bf16[8,8,256]{2,1,0:T(8,128)(2,1)S(1)}, u32[]{:S(2)}, u32[]{:S(2)}) collective-permute-start(bf16[8,8,256]{2,1,0:T(8,128)(2,1)S(1)} %get-tuple-element.25), channel_id=1, source_target_pairs={{0,24},{8,0},{16,8},{24,16},{1,25},{9,1},{17,9},{25,17},{2,26},{10... | collective-permute-start | bytes 98312 | tf_op jit(solution)/shard_map/ppermute | solution.py:37
  224.3 14.9 %all-to-all-start.2 = ((bf16[8,4,8,256]{3,2,1,0:T(8,128)(2,1)}), bf16[8,4,8,256]{3,2,1,0:T(8,128)(2,1)S(1)}, u32[]{:S(2)}, u32[]{:S(2)}) async-start(bf16[8,4,8,256]{3,2,1,0:T(8,128)(2,1)} %pad_maximum_fusion.1), calls=%async_computation.2 | async-start | bytes 262144 | tf_op jit(solution)/shard_map/all_to_all | solution.py:39
  241.0 6.3 %collective-permute-start.6 = (f32[40,136]{1,0:T(8,128)S(1)}, f32[40,136]{1,0:T(8,128)S(1)}, u32[]{:S(2)}, u32[]{:S(2)}) collective-permute-start(f32[40,136]{1,0:T(8,128)S(1)} %pad_maximum_fusion.2), channel_id=1, source_target_pairs={{0,512},{512,0},{1,513},{513,1},{2,514},{514,2},{3,515},{515,3},{4... | collective-permute-start | bytes 65288 | tf_op jit(solution)/shard_map/ppermute | solution.py:138
Sparse Core Ops, SparseCore 0:
  87.8 49.6 all-gather.1

commit v4 on v2

--- a/solution.py
+++ b/solution.py
@@ -84,43 +84,45 @@
         d_up, up_shard, preferred_element_type=jnp.float32
     )
     d_rows = d_rows.astype(jnp.bfloat16)
-    d_split = d_rows.reshape(slots, group_size, shard_count, out_width).transpose(2, 0, 1, 3)
-    d_split = d_split.reshape(shard_count, slots, chunk)
-    pad_rows = (-(slots + 1)) % 16 + 1
-    inner_row = jnp.pad(inner, (0, chunk - slots)).reshape(1, 1, chunk)
-    inner_row = jnp.broadcast_to(inner_row, (shard_count, 1, chunk))
+    dp_count = group_size * shard_count
+    d_split = d_rows.reshape(slots, dp_count, out_width).transpose(1, 0, 2)
+    inner_rows = -(-slots // out_width)
+    pad_rows = (-(slots + inner_rows)) % 16
+    inner_block = jnp.pad(inner, (0, inner_rows * out_width - slots)).reshape(1, inner_rows, out_width)
     extra = jnp.concatenate(
-        [inner_row, jnp.zeros((shard_count, pad_rows - 1, chunk), jnp.bfloat16)], axis=1
+        [inner_block, jnp.zeros((1, pad_rows, out_width), jnp.bfloat16)], axis=1
     )
+    extra = jnp.broadcast_to(extra, (dp_count,) + extra.shape[1:])
     ex_send = jnp.concatenate([d_split, extra], axis=1)
-    ex_recv = lax.all_to_all(ex_send, "s", split_axis=0, concat_axis=0, tiled=True)
-    summed = jnp.sum(ex_recv.astype(jnp.float32), axis=0)
-    grads_chunk = summed[:slots].reshape(dest_count, send_rows, chunk)
-    inner_sum = summed[slots, :slots].reshape(dest_count, send_rows)
+    ex_recv = lax.all_to_all(ex_send, ("l", "s"), split_axis=0, concat_axis=0, tiled=True)
+    ex_recv = ex_recv.reshape((group_size, shard_count) + ex_recv.shape[1:])
+    summed = jnp.sum(ex_recv.astype(jnp.float32), axis=1)
+    grads_chunk = summed[:, :slots].reshape(group_size, dest_count, send_rows, out_width)
+    grads_chunk = grads_chunk.transpose(1, 0, 2, 3).astype(jnp.bfloat16)
+    inner_sum = summed[:, slots:slots + inner_rows].reshape(group_size, inner_rows * out_width)
+    inner_sum = inner_sum[:, :slots].reshape(group_size, dest_count, send_rows).transpose(1, 0, 2)
     inner_hi = inner_sum.astype(jnp.bfloat16)
     inner_lo = (inner_sum - inner_hi.astype(jnp.float32)).astype(jnp.bfloat16)
-    inner_pair = jnp.concatenate([inner_hi, inner_lo], axis=1).reshape(dest_count, 1, 2 * send_rows)
-    inner_pair = jnp.pad(inner_pair, ((0, 0), (0, 0), (0, chunk - 2 * send_rows)))
-    back_send = jnp.concatenate([grads_chunk.astype(jnp.bfloat16), inner_pair], axis=1)
+    inner_pair = jnp.concatenate([inner_hi, inner_lo], axis=2).reshape(dest_count, group_size, 1, 2 * send_rows)
+    inner_pair = jnp.pad(inner_pair, ((0, 0), (0, 0), (0, 0), (0, out_width - 2 * send_rows)))
+    back_send = jnp.concatenate([grads_chunk, inner_pair], axis=2)
     back = lax.all_to_all(back_send, "expert", split_axis=0, concat_axis=0, tiled=True)
 
-    grads_back = back[:, :send_rows, :].reshape(slots, chunk)
-    inner_back = back[:, send_rows, :2 * send_rows].astype(jnp.float32)
-    inner_back = (inner_back[:, :send_rows] + inner_back[:, send_rows:]).reshape(slots)
+    back = back.transpose(1, 0, 2, 3)
+    grads_back = back[:, :, :send_rows, :].reshape(group_size * slots, out_width)
+    inner_back = back[:, :, send_rows, :2 * send_rows].astype(jnp.float32)
+    inner_back = (inner_back[:, :, :send_rows] + inner_back[:, :, send_rows:]).reshape(group_size * slots)
+    tables = [slot_tables(expert_ids, kind, group_size, dest_count, send_rows) for kind in range(group_size)]
+    placing_all = jnp.concatenate([t[0] for t in tables], axis=0)
+    by_token_all = jnp.concatenate([t[1] for t in tables], axis=0)
     contract_rows = (((0,), (0,)), ((), ()))
-    token_terms = lax.dot_general(
-        by_token, grads_back, contract_rows, preferred_element_type=jnp.float32
-    ).reshape(tok_rows, group_size, out_width)
-    slot_terms = lax.dot_general(
-        placing.astype(jnp.float32), inner_back, contract_rows,
+    d_tokens = lax.dot_general(
+        by_token_all, grads_back, contract_rows, preferred_element_type=jnp.float32
+    ).astype(jnp.bfloat16)
+    d_probs = lax.dot_general(
+        placing_all.astype(jnp.float32), inner_back, contract_rows,
         preferred_element_type=jnp.float32, precision=HIGH,
     ).reshape(tok_rows, TOP)
-    mine = lax.dynamic_index_in_dim(token_terms, shard_type, axis=1, keepdims=False)
-    other = lax.dynamic_index_in_dim(token_terms, 1 - shard_type, axis=1, keepdims=False)
-    pair_send = jnp.concatenate([other, slot_terms], axis=1)
-    pair_recv = lax.ppermute(pair_send, "l", perm=[(0, 1), (1, 0)])
-    d_tokens = (mine + pair_recv[:, :out_width]).astype(jnp.bfloat16)
-    d_probs = slot_terms + pair_recv[:, out_width:]
     return (d_tokens, d_probs)
 
 

time: 238 us -> 231 us (0.971); the launches traced: 235 us -> 231 us
  starting transfers between devices: 26.4 us -> 22.7 us
  local copies, waits for them, and re-layouts: 13 us -> 9.89 us
  blocking collectives: 99.4 us -> 102 us
    ppermute x1 -> x0, starting transfers between devices: 4.34 us -> none  [shards(): pair_recv = lax.ppermute(pair_send, 'l', perm=[(0, 1), (1, 0)])]
    reshape x5 -> x7, local copies, waits for them, and re-layouts: 4.1 us -> 0.81 us  [the longest x1 0.32 us: shards(): d_split = d_rows.reshape(slots, dp_count, out_width).transpose(1, 0, 2)]
    all_to_all x1, blocking collectives: 29.8 us -> 32.8 us  [shards(): lax.all_to_all(ex_send, ('l', 's'), split_axis=0, concat_axis=0, tiled=True)]
  transfers between devices with their start and end apart: 3 -> 2, of which waited for: 3 -> 2; matrix products, arithmetic and copies ran while one was open for 0% -> 0% of each run, Pallas kernels for 0% -> 0%
where the time goes in v4:
time: 231 us
  blocking collectives  102 us (44%)
  waiting for transfers between devices  67.7 us (29%)
  starting transfers between devices  22.7 us (10%)
  between operations  14.5 us (6%)
  local copies, waits for them, and re-layouts  9.89 us (4%)
  matrix products  7.75 us (3%)
  other arithmetic  5.97 us (3%)
    all_to_all x1, blocking collectives, shards(): lax.all_to_all(payload, 'expert', split_axis=0, concat_axis=0, tiled=True)  69.6 us
    all_gather x1, waiting for transfers between devices, shards(): gathered = lax.all_gather(rows_in, 's', axis=0, tiled=False)  38.5 us
    all_to_all x1, blocking collectives, shards(): lax.all_to_all(ex_send, ('l', 's'), split_axis=0, concat_axis=0, tiled=True)  32.8 us
    all_to_all x1, waiting for transfers between devices, shards(): lax.all_to_all(back_send, 'expert', split_axis=0, concat_axis=0, tiled=True)  29.2 us
    all_to_all x1, starting transfers between devices, shards(): lax.all_to_all(back_send, 'expert', split_axis=0, concat_axis=0, tiled=True)  22.6 us
    unnamed x11, local copies, waits for them, and re-layouts  4.81 us
  transfers between devices with their start and end apart: 2, of which 2 were waited for; matrix products, arithmetic and copies ran while one was open for 0% of the time, Pallas kernels for 0%

profile of v4, /device:TPU:1, one launch (start us, length us, event | category | flops | bytes accessed | tf_op | source)
XLA Modules:
  0.0 230.8 jit_solution(5588979495394039935)
XLA Ops:
  7.2 0.8 copy.115
  8.2 0.9 reduce-window.20
  9.5 0.9 reduce-window.26
  10.7 0.9 reduce-window.24
  12.3 0.8 copy.126
  13.7 0.8 constant_dynamic-slice_fusion
  14.9 69.6 %all_to_all.15 = bf16[32,8,512]{2,1,0:T(8,128)(2,1)S(1)} all-to-all(bf16[32,8,512]{2,1,0:T(8,128)(2,1)S(1)} %fusion.17), channel_id=1, replica_groups=mesh['l'=2,'s'=16,'expert'=32] {'expert'}, dimensions={0} | all-to-all | bytes 524288 | tf_op jit(solution)/shard_map/all_to_all | solution.py:54
  84.5 0.8 all_gather_reshape.3
  85.5 38.5 %all-gather.2.cloned.1.call-done = bf16[16,224,512]{2,1,0:T(8,128)(2,1)} async-done(((bf16[1,224,512]{2,1,0:T(8,128)(2,1)}), bf16[16,224,512]{2,1,0:T(8,128)(2,1)}) %all-gather.2.cloned.1.call-update) | async-done | bytes 3670032 | tf_op jit(solution)/shard_map/all_gather | solution.py:58
  124.0 2.3 slice_bitcast_fusion.1
  126.8 0.9 copy-done.1
  127.7 0.7 fusion.4
  128.4 0.7 fusion.7
  129.1 0.7 convolution_convert_fusion
  129.8 0.7 convolution_multiply_fusion
  131.1 0.7 fusion.2
  131.8 0.7 fusion.1
  133.0 32.8 %all_to_all.16 = bf16[32,240,128]{2,1,0:T(8,128)(2,1)S(1)} all-to-all(bf16[32,240,128]{2,1,0:T(8,128)(2,1)S(1)} %pad_maximum_fusion), channel_id=1, replica_groups=mesh['l'=2,'s'=16,'expert'=32] {'l','s'}, dimensions={0} | all-to-all | bytes 3932160 | tf_op jit(solution)/shard_map/all_to_all | solution.py:97
  166.5 0.8 fusion.22
  167.3 22.6 %all-to-all-start.2 = ((bf16[32,2,8,128]{3,1,2,0:T(2,128)(2,1)}), bf16[32,2,8,128]{3,1,2,0:T(2,128)(2,1)S(1)}, u32[]{:S(2)}, u32[]{:S(2)}) async-start(bf16[32,2,8,128]{3,1,2,0:T(2,128)(2,1)} %fusion.22), calls=%async_computation.2 | async-start | bytes 262144 | tf_op jit(solution)/shard_map/all_to_all | solution.py:109
  190.5 29.2 %all-to-all-done.2 = bf16[32,2,8,128]{3,1,2,0:T(2,128)(2,1)S(1)} async-done(((bf16[32,2,8,128]{3,1,2,0:T(2,128)(2,1)}), bf16[32,2,8,128]{3,1,2,0:T(2,128)(2,1)S(1)}, u32[]{:S(2)}, u32[]{:S(2)}) %all-to-all-start.2) | async-done | bytes 131104 | tf_op jit(solution)/shard_map/all_to_all | solution.py:109
  220.1 2.3 %fusion.11 = f32[1,40,8]{2,0,1:T(1,128)S(1)} fusion(f32[448,1,1]{0,1,2:T(1,128)S(1)} %reshape.307, pred[224,320]{0,1:T(32,128)(4,1)S(1)} %iota_compare_fusion.3, pred[224,320]{0,1:T(32,128)(4,1)S(1)} %iota_compare_fusion.4), kind=kOutput, calls=%fused_computation.23 | convolution fusion | flops 1863680 | bytes 146432 | tf_op jit(solution)/shard_map/dot_general | solution.py:122
  222.4 0.7 copy.136
  223.2 0.8 convolution_convert_fusion.2
  (70 shorter events, 5.9 us)
Async XLA Ops:
  7.2 122.0 %copy-start = (bf16[1,96,4096]{2,1,0:T(8,128)(2,1)S(1)}, bf16[1,96,4096]{2,1,0:T(8,128)(2,1)}, u32[]{:S(2)}) copy-start(bf16[1,96,4096]{2,1,0:T(8,128)(2,1)} %param.13) | copy-start | bytes 2359300
  7.2 116.8 %all-gather.2.cloned.1.call-start = ((), (), s32[]{:S(2)}) async-start(), calls=%async_computation.3 | async-start | bytes 3899392 | tf_op jit(solution)/shard_map/all_gather | solution.py:58
  126.5 1.1 copy-start.1
  126.8 1.6 copy-start.2
  167.3 52.4 %all-to-all-start.2 = ((bf16[32,2,8,128]{3,1,2,0:T(2,128)(2,1)}), bf16[32,2,8,128]{3,1,2,0:T(2,128)(2,1)S(1)}, u32[]{:S(2)}, u32[]{:S(2)}) async-start(bf16[32,2,8,128]{3,1,2,0:T(2,128)(2,1)} %fusion.22), calls=%async_computation.2 | async-start | bytes 262144 | tf_op jit(solution)/shard_map/all_to_all | solution.py:109
Sparse Core Ops, SparseCore 0:
  85.4 38.5 all-gather.1

commit v5 on v4

--- a/solution.py
+++ b/solution.py
@@ -7,7 +7,6 @@
 FF = 1536
 TOP = 8
 GROUP = 2
-HIGH = lax.Precision.HIGHEST
 
 
 def slot_tables(expert_ids, shard_type, group_size, dest_count, send_rows):
@@ -31,7 +30,8 @@
     shard_count = FF // shard_width
     group_size = lax.axis_size("l")
     shard_type = lax.axis_index("l")
-    part = lax.axis_index("s")
+    part = (lax.axis_index("sy") * lax.axis_size("sx") + lax.axis_index("sx")) * lax.axis_size("c") + lax.axis_index("c")
+    core = lax.axis_index("c")
     tok_rows = tokens.shape[0]
     model_width = tokens.shape[1]
     chunk = model_width // shard_count
@@ -39,7 +39,11 @@
     experts_all = group_size * dest_count
     send_rows = (4 * tok_rows * TOP + 3 * experts_all - 1) // (3 * experts_all)
     slots = dest_count * send_rows
-    placing, by_token = slot_tables(expert_ids, shard_type, group_size, dest_count, send_rows)
+    tables = [slot_tables(expert_ids, kind, group_size, dest_count, send_rows) for kind in range(group_size)]
+    placing_all = jnp.concatenate([t[0] for t in tables], axis=0)
+    by_token_all = jnp.concatenate([t[1] for t in tables], axis=0)
+    placing = lax.dynamic_slice_in_dim(placing_all, shard_type * slots, slots, axis=0)
+    by_token = lax.dynamic_slice_in_dim(by_token_all, shard_type * slots, slots, axis=0)
 
     tok_chunk = lax.dynamic_slice_in_dim(tokens, part * chunk, chunk, axis=1)
     cot_chunk = lax.dynamic_slice_in_dim(cotangent, part * chunk, chunk, axis=1)
@@ -55,7 +59,12 @@
     probs_in = recv[:, send_rows, :send_rows].reshape(slots).astype(jnp.float32)
     rows_in = recv[:, :send_rows, :].reshape(slots, 2 * chunk)
 
-    gathered = lax.all_gather(rows_in, "s", axis=0, tiled=False)
+    chips = lax.axis_size("sy") * lax.axis_size("sx")
+    spread = jnp.broadcast_to(rows_in[None], (chips,) + rows_in.shape)
+    same_core = lax.all_to_all(spread, ("sy", "sx"), split_axis=0, concat_axis=0, tiled=True)
+    other_core = lax.ppermute(same_core, "c", perm=[(0, 1), (1, 0)])
+    by_core = jnp.stack([same_core, other_core, same_core], axis=1)
+    gathered = lax.dynamic_slice_in_dim(by_core, core, 2, axis=1).reshape((shard_count,) + rows_in.shape)
     tok_parts = gathered[:, :, :chunk]
     cot_parts = gathered[:, :, chunk:]
     rows_tok = tok_parts.transpose(1, 0, 2).reshape(slots, model_width)
@@ -94,7 +103,7 @@
     )
     extra = jnp.broadcast_to(extra, (dp_count,) + extra.shape[1:])
     ex_send = jnp.concatenate([d_split, extra], axis=1)
-    ex_recv = lax.all_to_all(ex_send, ("l", "s"), split_axis=0, concat_axis=0, tiled=True)
+    ex_recv = lax.all_to_all(ex_send, ("l", "sy", "sx", "c"), split_axis=0, concat_axis=0, tiled=True)
     ex_recv = ex_recv.reshape((group_size, shard_count) + ex_recv.shape[1:])
     summed = jnp.sum(ex_recv.astype(jnp.float32), axis=1)
     grads_chunk = summed[:, :slots].reshape(group_size, dest_count, send_rows, out_width)
@@ -110,19 +119,17 @@
 
     back = back.transpose(1, 0, 2, 3)
     grads_back = back[:, :, :send_rows, :].reshape(group_size * slots, out_width)
-    inner_back = back[:, :, send_rows, :2 * send_rows].astype(jnp.float32)
-    inner_back = (inner_back[:, :, :send_rows] + inner_back[:, :, send_rows:]).reshape(group_size * slots)
-    tables = [slot_tables(expert_ids, kind, group_size, dest_count, send_rows) for kind in range(group_size)]
-    placing_all = jnp.concatenate([t[0] for t in tables], axis=0)
-    by_token_all = jnp.concatenate([t[1] for t in tables], axis=0)
+    inner_back = back[:, :, send_rows, :2 * send_rows]
+    inner_hi = inner_back[:, :, :send_rows].reshape(group_size * slots)
+    inner_lo = inner_back[:, :, send_rows:].reshape(group_size * slots)
     contract_rows = (((0,), (0,)), ((), ()))
     d_tokens = lax.dot_general(
         by_token_all, grads_back, contract_rows, preferred_element_type=jnp.float32
     ).astype(jnp.bfloat16)
     d_probs = lax.dot_general(
-        placing_all.astype(jnp.float32), inner_back, contract_rows,
-        preferred_element_type=jnp.float32, precision=HIGH,
-    ).reshape(tok_rows, TOP)
+        placing_all, inner_hi, contract_rows, preferred_element_type=jnp.float32
+    ) + lax.dot_general(placing_all, inner_lo, contract_rows, preferred_element_type=jnp.float32)
+    d_probs = d_probs.reshape(tok_rows, TOP)
     return (d_tokens, d_probs)
 
 
@@ -132,7 +139,9 @@
     if names != ("dp", "expert"):
         devices = devices.transpose([names.index("dp"), names.index("expert")])
     dp_size = devices.shape[0]
-    split = Mesh(devices.reshape(GROUP, dp_size // GROUP, devices.shape[1]), ("l", "s", "expert"))
+    split = Mesh(
+        devices.reshape(GROUP, 2, dp_size // (4 * GROUP), 2, devices.shape[1]), ("l", "sy", "sx", "c", "expert")
+    )
     return jax.shard_map(
         shards,
         mesh=split,
@@ -141,10 +150,10 @@
             P("expert", None),
             P("expert", None),
             P("expert", None),
-            P("expert", ("l", "s"), None),
-            P("expert", ("l", "s"), None),
-            P("expert", ("l", "s"), None),
+            P("expert", ("l", "sy", "sx", "c"), None),
+            P("expert", ("l", "sy", "sx", "c"), None),
+            P("expert", ("l", "sy", "sx", "c"), None),
         ),
-        out_specs=(P("expert", ("l", "s")), P("expert", None)),
+        out_specs=(P("expert", ("l", "sy", "sx", "c")), P("expert", None)),
         check_vma=False,
     )

time: 231 us -> 193 us (0.84)
  waiting for transfers between devices: 67.7 us -> 3.35 us
  blocking collectives: 102 us -> 162 us
  starting transfers between devices: 22.7 us -> 5.77 us
  between operations: 14.5 us -> 1.08 us
    all_to_all x1 -> x3, blocking collectives: 32.8 us -> 91.9 us  [the longest x1 33.8 us: shards(): lax.all_to_all(back_send, 'expert', split_axis=0, concat_axis=0, tiled=True)]
    all_gather x1 -> x0, waiting for transfers between devices: 38.5 us -> none  [shards(): gathered = lax.all_gather(rows_in, 's', axis=0, tiled=False)]
    all_to_all x1 -> x0, waiting for transfers between devices: 29.2 us -> none  [shards(): lax.all_to_all(back_send, 'expert', split_axis=0, concat_axis=0, tiled=True)]
    all_to_all x1 -> x0, starting transfers between devices: 22.6 us -> none  [shards(): lax.all_to_all(back_send, 'expert', split_axis=0, concat_axis=0, tiled=True)]
    ppermute x0 -> x1, starting transfers between devices: none -> 5.77 us  [shards(): other_core = lax.ppermute(same_core, 'c', perm=[(0, 1), (1, 0)])]
    ppermute x0 -> x1, waiting for transfers between devices: none -> 3.35 us  [shards(): other_core = lax.ppermute(same_core, 'c', perm=[(0, 1), (1, 0)])]
    another operation x10 -> x7, other arithmetic: 3 us -> 5.2 us  [the longest x1 3.2 us: shards(): by_core = jnp.stack([same_core, other_core, same_core], axis=1)]
    unnamed x11 -> x12, local copies, waits for them, and re-layouts: 4.81 us -> 3.48 us
  transfers between devices with their start and end apart: 2 -> 1, of which waited for: 2 -> 1; matrix products, arithmetic and copies ran while one was open for 0% -> 0% of each run, Pallas kernels for 0% -> 0%
where the time goes in v5:
time: 193 us
  blocking collectives  162 us (84%)
  local copies, waits for them, and re-layouts  7.96 us (4%)
  other arithmetic  7.08 us (4%)
  matrix products  6 us (3%)
  starting transfers between devices  5.77 us (3%)
  waiting for transfers between devices  3.35 us (2%)
    all_to_all x1, blocking collectives, shards(): lax.all_to_all(payload, 'expert', split_axis=0, concat_axis=0, tiled=True)  69.6 us
    all_to_all x1, blocking collectives, shards(): lax.all_to_all(back_send, 'expert', split_axis=0, concat_axis=0, tiled=True)  33.8 us
    all_to_all x1, blocking collectives, shards(): lax.all_to_all(ex_send, ('l', 'sy', 'sx', 'c'), split_axis=0, concat_axis...  32.1 us
    all_to_all x1, blocking collectives, shards(): lax.all_to_all(spread, ('sy', 'sx'), split_axis=0, concat_axis=0, tiled=T...  26 us
    ppermute x1, starting transfers between devices, shards(): other_core = lax.ppermute(same_core, 'c', perm=[(0, 1), (1, 0)])  5.77 us
  transfers between devices with their start and end apart: 1, of which 1 were waited for; matrix products, arithmetic and copies ran while one was open for 0% of the time, Pallas kernels for 0%

profile of v5, /device:TPU:1, one launch (start us, length us, event | category | flops | bytes accessed | tf_op | source)
XLA Modules:
  0.0 192.8 jit_solution(14864762051557601434)
XLA Ops:
  0.6 0.8 copy.142
  1.7 0.9 reduce-window.16
  2.9 0.9 reduce-window.14
  4.4 0.8 copy.151
  6.2 0.8 constant_dynamic-slice_fusion
  6.9 0.3 convolution_convert_fusion.1
  7.5 69.6 %all_to_all.20 = bf16[32,8,512]{2,1,0:T(8,128)(2,1)S(1)} all-to-all(bf16[32,8,512]{2,1,0:T(8,128)(2,1)S(1)} %fusion.19), channel_id=1, replica_groups=mesh['l'=2,'sy'=2,'sx'=4,'c'=2,'expert'=32] {'expert'}, dimensions={0} | all-to-all | bytes 524288 | tf_op jit(solution)/shard_map/all_to_all | solution.py:58
  77.3 26.0 %all_to_all.21 = bf16[8,224,512]{2,1,0:T(8,128)(2,1)S(1)} all-to-all(bf16[8,224,512]{2,1,0:T(8,128)(2,1)S(1)} %broadcast_in_dim.12), channel_id=1, replica_groups=mesh['l'=2,'sy'=2,'sx'=4,'c'=2,'expert'=32] {'sy','sx'}, dimensions={0} | all-to-all | bytes 3670016 | tf_op jit(solution)/shard_map/all_to_all | solution.py:64
  103.4 5.8 %collective-permute-start = (bf16[8,224,512]{2,1,0:T(8,128)(2,1)S(1)}, bf16[8,224,512]{2,1,0:T(8,128)(2,1)}, u32[]{:S(2)}, u32[]{:S(2)}) collective-permute-start(bf16[8,224,512]{2,1,0:T(8,128)(2,1)S(1)} %all_to_all.21), channel_id=1, source_target_pairs={{0,32},{32,0},{1,33},{33,1},{2,34},{34,2},{3,35},{35,3},{4,36},{36... | collective-permute-start | bytes 5505032 | tf_op jit(solution)/shard_map/ppermute | solution.py:65
  109.3 3.4 %collective-permute-done = bf16[8,224,512]{2,1,0:T(8,128)(2,1)} collective-permute-done((bf16[8,224,512]{2,1,0:T(8,128)(2,1)S(1)}, bf16[8,224,512]{2,1,0:T(8,128)(2,1)}, u32[]{:S(2)}, u32[]{:S(2)}) %collective-permute-start) | collective-permute-done | bytes 1835040 | tf_op jit(solution)/shard_map/ppermute | solution.py:65
  112.7 3.2 %fusion.2 = bf16[8,2,224,512]{3,2,0,1:T(8,128)(2,1)S(1)} fusion(s32[]{:T(128)S(6)} %select_n.90, bf16[8,1,224,512]{3,2,0,1:T(8,128)(2,1)S(1)} %bitcast.101, bf16[8,1,224,512]{3,2,0,1:T(8,128)(2,1)} %bitcast.4), kind=kLoop, calls=%fused_computation.8 | loop fusion | flops 3670016 | bytes 7340036 | tf_op jit(solution)/shard_map/stack | solution.py:66
  115.9 0.3 copy.153
  117.0 0.9 copy-done.1
  117.9 0.7 fusion.6
  118.6 0.7 fusion.9
  119.3 0.7 convolution_convert_fusion
  120.0 0.7 convolution_multiply_fusion
  120.7 0.6 multiply_reduce_fusion
  121.3 0.7 fusion.4
  122.0 0.7 fusion.3
  123.2 32.1 %all_to_all.22 = bf16[32,240,128]{2,1,0:T(8,128)(2,1)S(1)} all-to-all(bf16[32,240,128]{2,1,0:T(8,128)(2,1)S(1)} %pad_maximum_fusion), channel_id=1, replica_groups=mesh['l'=2,'sy'=2,'sx'=4,'c'=2,'expert'=32] {'l','sy','sx','c'}, dimensions={0} | all-to-all | bytes 3932160 | tf_op jit(solution)/shard_map/all_to_all | solution.py:106
  156.1 33.8 %all_to_all.23 = bf16[32,2,8,128]{3,1,2,0:T(2,128)(2,1)S(1)} all-to-all(bf16[32,2,8,128]{3,1,2,0:T(2,128)(2,1)S(1)} %fusion.22), channel_id=1, replica_groups=mesh['l'=2,'sy'=2,'sx'=4,'c'=2,'expert'=32] {'expert'}, dimensions={0} | all-to-all | bytes 262144 | tf_op jit(solution)/shard_map/all_to_all | solution.py:118
  191.2 0.8 convolution_convert_fusion.2
  192.1 0.7 copy.164
  (70 shorter events, 5.9 us)
Async XLA Ops:
  0.6 118.7 %copy-start = (bf16[1,96,4096]{2,1,0:T(8,128)(2,1)S(1)}, bf16[1,96,4096]{2,1,0:T(8,128)(2,1)}, u32[]{:S(2)}) copy-start(bf16[1,96,4096]{2,1,0:T(8,128)(2,1)} %param.13) | copy-start | bytes 2359300
  103.4 9.3 %collective-permute-start = (bf16[8,224,512]{2,1,0:T(8,128)(2,1)S(1)}, bf16[8,224,512]{2,1,0:T(8,128)(2,1)}, u32[]{:S(2)}, u32[]{:S(2)}) collective-permute-start(bf16[8,224,512]{2,1,0:T(8,128)(2,1)S(1)} %all_to_all.21), channel_id=1, source_target_pairs={{0,32},{32,0},{1,33},{33,1},{2,34},{34,2},{3,35},{35,3},{4,36},{36... | collective-permute-start | bytes 5505032 | tf_op jit(solution)/shard_map/ppermute | solution.py:65
  116.7 1.1 copy-start.1
  117.0 1.6 copy-start.2

commit v6 on v5

--- a/solution.py
+++ b/solution.py
@@ -94,22 +94,35 @@
     )
     d_rows = d_rows.astype(jnp.bfloat16)
     dp_count = group_size * shard_count
-    d_split = d_rows.reshape(slots, dp_count, out_width).transpose(1, 0, 2)
+    cores = lax.axis_size("c")
+    d_view = d_rows.reshape(slots, dp_count // cores, cores, out_width)
+    keep = lax.dynamic_index_in_dim(d_view, core, axis=2, keepdims=False)
+    give = lax.dynamic_index_in_dim(d_view, 1 - core, axis=2, keepdims=False)
+    swap = [(0, 1), (1, 0)]
+    got = lax.ppermute(give, "c", perm=swap)
+    inner_peer = lax.ppermute(inner, "c", perm=swap)
+    pair_sum = (keep.astype(jnp.float32) + got.astype(jnp.float32)).astype(jnp.bfloat16)
+    d_split = pair_sum.transpose(1, 0, 2)
     inner_rows = -(-slots // out_width)
-    pad_rows = (-(slots + inner_rows)) % 16
-    inner_block = jnp.pad(inner, (0, inner_rows * out_width - slots)).reshape(1, inner_rows, out_width)
+    inner_both = jnp.where(core == 0, jnp.stack([inner, inner_peer]), jnp.stack([inner_peer, inner]))
+    inner_block = jnp.pad(inner_both, ((0, 0), (0, inner_rows * out_width - slots)))
+    inner_block = inner_block.reshape(1, cores * inner_rows, out_width)
+    pad_rows = (-(slots + cores * inner_rows)) % 16
     extra = jnp.concatenate(
         [inner_block, jnp.zeros((1, pad_rows, out_width), jnp.bfloat16)], axis=1
     )
-    extra = jnp.broadcast_to(extra, (dp_count,) + extra.shape[1:])
+    extra = jnp.broadcast_to(extra, (dp_count // cores,) + extra.shape[1:])
     ex_send = jnp.concatenate([d_split, extra], axis=1)
-    ex_recv = lax.all_to_all(ex_send, ("l", "sy", "sx", "c"), split_axis=0, concat_axis=0, tiled=True)
-    ex_recv = ex_recv.reshape((group_size, shard_count) + ex_recv.shape[1:])
-    summed = jnp.sum(ex_recv.astype(jnp.float32), axis=1)
-    grads_chunk = summed[:, :slots].reshape(group_size, dest_count, send_rows, out_width)
+    ex_recv = lax.all_to_all(ex_send, ("l", "sy", "sx"), split_axis=0, concat_axis=0, tiled=True)
+    ex_recv = ex_recv.reshape((group_size, shard_count // cores) + ex_recv.shape[1:]).astype(jnp.float32)
+    grads_sum = jnp.sum(ex_recv[:, :, :slots], axis=1)
+    inner_parts = ex_recv[:, :, slots:slots + cores * inner_rows].reshape(
+        group_size, shard_count // cores, cores, inner_rows * out_width
+    )
+    inner_sum = jnp.sum(inner_parts, axis=(1, 2))[:, :slots]
+    grads_chunk = grads_sum.reshape(group_size, dest_count, send_rows, out_width)
     grads_chunk = grads_chunk.transpose(1, 0, 2, 3).astype(jnp.bfloat16)
-    inner_sum = summed[:, slots:slots + inner_rows].reshape(group_size, inner_rows * out_width)
-    inner_sum = inner_sum[:, :slots].reshape(group_size, dest_count, send_rows).transpose(1, 0, 2)
+    inner_sum = inner_sum.reshape(group_size, dest_count, send_rows).transpose(1, 0, 2)
     inner_hi = inner_sum.astype(jnp.bfloat16)
     inner_lo = (inner_sum - inner_hi.astype(jnp.float32)).astype(jnp.bfloat16)
     inner_pair = jnp.concatenate([inner_hi, inner_lo], axis=2).reshape(dest_count, group_size, 1, 2 * send_rows)

time: 193 us -> 204 us (1.057); the launches traced: 193 us -> 202 us
  blocking collectives: 162 us -> 148 us
  local copies, waits for them, and re-layouts: 7.96 us -> 21.4 us
  starting transfers between devices: 5.77 us -> 10.3 us
    all_to_all x1, blocking collectives: 32.1 us -> 20.1 us  [shards(): lax.all_to_all(ex_send, ('l', 'sy', 'sx'), split_axis=0, concat_axis=0, t...]
    dynamic_slice x0 -> x1, local copies, waits for them, and re-layouts: none -> 7.08 us  [shards(): keep = lax.dynamic_index_in_dim(d_view, core, axis=2, keepdims=False)]
    reshape x4, local copies, waits for them, and re-layouts: 0.51 us -> 5.69 us  [the longest x1 5.48 us: shards(): d_view = d_rows.reshape(slots, dp_count // cores, cores, out_width)]
    ppermute x0 -> x2, starting transfers between devices: none -> 4.3 us  [the longest x1 2.28 us: shards(): got = lax.ppermute(give, 'c', perm=swap)]
    unnamed x12 -> x23, local copies, waits for them, and re-layouts: 3.48 us -> 4.46 us
  transfers between devices with their start and end apart: 1 -> 3, of which waited for: 1 -> 2; matrix products, arithmetic and copies ran while one was open for 0% -> 1% of each run, Pallas kernels for 0% -> 0%
where the time goes in v6:
time: 204 us; the launch traced here: 202 us
  blocking collectives  148 us (73%)
  local copies, waits for them, and re-layouts  21.4 us (10%)
  starting transfers between devices  10.3 us (5%)
  other arithmetic  9.02 us (4%)
  matrix products  7.28 us (4%)
  waiting for transfers between devices  4.13 us (2%)
    all_to_all x1, blocking collectives, shards(): lax.all_to_all(payload, 'expert', split_axis=0, concat_axis=0, tiled=True)  69.6 us
    all_to_all x1, blocking collectives, shards(): lax.all_to_all(back_send, 'expert', split_axis=0, concat_axis=0, tiled=True)  32.6 us
    all_to_all x1, blocking collectives, shards(): lax.all_to_all(spread, ('sy', 'sx'), split_axis=0, concat_axis=0, tiled=T...  26 us
    all_to_all x1, blocking collectives, shards(): lax.all_to_all(ex_send, ('l', 'sy', 'sx'), split_axis=0, concat_axis=0, t...  20.1 us
    dynamic_slice x1, local copies, waits for them, and re-layouts, shards(): keep = lax.dynamic_index_in_dim(d_view, core, axis=2, keepdims=False)  7.08 us
    ppermute x1, starting transfers between devices, shards(): other_core = lax.ppermute(same_core, 'c', perm=[(0, 1), (1, 0)])  5.97 us
    reshape x1, local copies, waits for them, and re-layouts, shards(): d_view = d_rows.reshape(slots, dp_count // cores, cores, out_width)  5.48 us
    unnamed x23, local copies, waits for them, and re-layouts  4.46 us
  transfers between devices with their start and end apart: 3, of which 2 were waited for; matrix products, arithmetic and copies ran while one was open for 1% of the time, Pallas kernels for 0%

profile of v6, /device:TPU:1, one launch (start us, length us, event | category | flops | bytes accessed | tf_op | source)
XLA Modules:
  0.0 201.7 jit_solution(4963880662296276307)
XLA Ops:
  0.6 0.8 copy.186
  1.7 0.9 reduce-window.16
  2.9 0.9 reduce-window.14
  4.4 0.8 copy.195
  6.2 0.8 constant_dynamic-slice_fusion.2
  7.5 69.6 %all_to_all.20 = bf16[32,8,512]{2,1,0:T(8,128)(2,1)S(1)} all-to-all(bf16[32,8,512]{2,1,0:T(8,128)(2,1)S(1)} %fusion.20), channel_id=1, replica_groups=mesh['l'=2,'sy'=2,'sx'=4,'c'=2,'expert'=32] {'expert'}, dimensions={0} | all-to-all | bytes 524288 | tf_op jit(solution)/shard_map/all_to_all | solution.py:58
  77.4 26.0 %all_to_all.21 = bf16[8,224,512]{2,1,0:T(8,128)(2,1)S(1)} all-to-all(bf16[8,224,512]{2,1,0:T(8,128)(2,1)S(1)} %broadcast_in_dim.12), channel_id=1, replica_groups=mesh['l'=2,'sy'=2,'sx'=4,'c'=2,'expert'=32] {'sy','sx'}, dimensions={0} | all-to-all | bytes 3670016 | tf_op jit(solution)/shard_map/all_to_all | solution.py:64
  103.4 6.0 %collective-permute-start = (bf16[8,224,512]{2,1,0:T(8,128)(2,1)S(1)}, bf16[8,224,512]{2,1,0:T(8,128)(2,1)}, u32[]{:S(2)}, u32[]{:S(2)}) collective-permute-start(bf16[8,224,512]{2,1,0:T(8,128)(2,1)S(1)} %all_to_all.21), channel_id=1, source_target_pairs={{0,32},{32,0},{1,33},{33,1},{2,34},{34,2},{3,35},{35,3},{4,36},{36... | collective-permute-start | bytes 5505032 | tf_op jit(solution)/shard_map/ppermute | solution.py:65
  109.5 3.2 %collective-permute-done = bf16[8,224,512]{2,1,0:T(8,128)(2,1)} collective-permute-done((bf16[8,224,512]{2,1,0:T(8,128)(2,1)S(1)}, bf16[8,224,512]{2,1,0:T(8,128)(2,1)}, u32[]{:S(2)}, u32[]{:S(2)}) %collective-permute-start) | collective-permute-done | bytes 1835040 | tf_op jit(solution)/shard_map/ppermute | solution.py:65
  112.7 3.2 %fusion.2 = bf16[8,2,224,512]{3,2,0,1:T(8,128)(2,1)S(1)} fusion(s32[]{:T(128)S(6)} %select_n.105, bf16[8,1,224,512]{3,2,0,1:T(8,128)(2,1)S(1)} %bitcast.95, bf16[8,1,224,512]{3,2,0,1:T(8,128)(2,1)} %bitcast.4), kind=kLoop, calls=%fused_computation.7 | loop fusion | flops 3670016 | bytes 7340036 | tf_op jit(solution)/shard_map/stack | solution.py:66
  117.0 0.7 fusion.7
  118.1 0.7 fusion.10
  119.2 0.7 convolution_multiply_fusion
  120.6 1.9 fusion
  122.6 5.5 %reshape.257 = bf16[224,16,2,128]{3,2,1,0:T(2,128)(2,1)} reshape(bf16[224,4096]{1,0:T(8,128)(2,1)} %fusion) | data formatting | bytes 3670016 | tf_op jit(solution)/shard_map/reshape | solution.py:98
  128.1 7.1 %constant_dynamic-slice_fusion.1 = (bf16[224,16,1,128]{3,2,1,0:T(2,128)(2,1)}, bf16[224,16,1,128]{3,2,1,0:T(2,128)(2,1)S(1)}) fusion(bf16[224,16,2,128]{3,2,1,0:T(2,128)(2,1)} %reshape.257, s32[]{:T(128)S(6)} %select_n.106, s32[]{:T(128)S(6)} %select_n.107), kind=kLoop, calls=%fused_computation.110 | loop fusion | bytes 3670024 | tf_op jit(solution)/shard_map/jit(dynamic_index_in_dim)/dynamic_slice | solution.py:99
  135.1 1.1 copy.231
  136.2 2.3 %collective-permute-start.1 = (bf16[224,16,128]{2,1,0:T(8,128)(2,1)}, bf16[224,16,128]{2,1,0:T(8,128)(2,1)}, u32[]{:S(2)}, u32[]{:S(2)}) collective-permute-start(bf16[224,16,128]{2,1,0:T(8,128)(2,1)} %bitcast.83), channel_id=1, source_target_pairs={{0,32},{32,0},{1,33},{33,1},{2,34},{34,2},{3,35},{35,3},{4,36},{36... | collective-permute-start | bytes 2752520 | tf_op jit(solution)/shard_map/ppermute | solution.py:102
  139.8 2.0 %collective-permute-start.2 = (bf16[224]{0:T(256)(128)(2,1)S(1)}, bf16[224]{0:T(256)(128)(2,1)S(1)}, u32[]{:S(2)}, u32[]{:S(2)}) collective-permute-start(bf16[224]{0:T(256)(128)(2,1)S(1)} %multiply_reduce_fusion), channel_id=1, source_target_pairs={{0,32},{32,0},{1,33},{33,1},{2,34},{34,2},{3,35},{35,3},{4,36},{36... | collective-permute-start | bytes 1352 | tf_op jit(solution)/shard_map/ppermute | solution.py:103
  141.8 1.0 collective-permute-done.2
  142.8 2.0 fusion.4
  145.2 20.1 %all_to_all.22 = bf16[16,240,128]{2,1,0:T(8,128)(2,1)S(1)} all-to-all(bf16[16,240,128]{2,1,0:T(8,128)(2,1)S(1)} %copy.202), channel_id=1, replica_groups=mesh['l'=2,'sy'=2,'sx'=4,'c'=2,'expert'=32] {'l','sy','sx'}, dimensions={0} | all-to-all | bytes 1966080 | tf_op jit(solution)/shard_map/all_to_all | solution.py:116
  166.2 32.6 %all_to_all.23 = bf16[32,2,8,128]{3,1,2,0:T(2,128)(2,1)S(1)} all-to-all(bf16[32,2,8,128]{3,1,2,0:T(2,128)(2,1)S(1)} %fusion.23), channel_id=1, replica_groups=mesh['l'=2,'sy'=2,'sx'=4,'c'=2,'expert'=32] {'expert'}, dimensions={0} | all-to-all | bytes 262144 | tf_op jit(solution)/shard_map/all_to_all | solution.py:131
  200.1 0.8 convolution_convert_fusion.2
  (95 shorter events, 9.9 us)
Async XLA Ops:
  0.6 116.3 %copy-start = (bf16[1,96,4096]{2,1,0:T(8,128)(2,1)S(1)}, bf16[1,96,4096]{2,1,0:T(8,128)(2,1)}, u32[]{:S(2)}) copy-start(bf16[1,96,4096]{2,1,0:T(8,128)(2,1)} %param.11) | copy-start | bytes 2359300
  5.7 1.2 copy-start.5
  5.8 1.1 copy-start.7
  103.4 9.3 %collective-permute-start = (bf16[8,224,512]{2,1,0:T(8,128)(2,1)S(1)}, bf16[8,224,512]{2,1,0:T(8,128)(2,1)}, u32[]{:S(2)}, u32[]{:S(2)}) collective-permute-start(bf16[8,224,512]{2,1,0:T(8,128)(2,1)S(1)} %all_to_all.21), channel_id=1, source_target_pairs={{0,32},{32,0},{1,33},{33,1},{2,34},{34,2},{3,35},{35,3},{4,36},{36... | collective-permute-start | bytes 5505032 | tf_op jit(solution)/shard_map/ppermute | solution.py:65
  117.0 1.1 copy-start.1
  118.1 1.1 copy-start.2
  118.8 1.1 copy-start.3
  135.1 3.4 %copy-start.4 = (f32[224,96]{0,1:T(8,128)S(1)}, f32[224,96]{0,1:T(8,128)}, u32[]{:S(2)}) copy-start(f32[224,96]{0,1:T(8,128)} %copy-done.3) | copy-start | bytes 258052
  136.2 6.6 %collective-permute-start.1 = (bf16[224,16,128]{2,1,0:T(8,128)(2,1)}, bf16[224,16,128]{2,1,0:T(8,128)(2,1)}, u32[]{:S(2)}, u32[]{:S(2)}) collective-permute-start(bf16[224,16,128]{2,1,0:T(8,128)(2,1)} %bitcast.83), channel_id=1, source_target_pairs={{0,32},{32,0},{1,33},{33,1},{2,34},{34,2},{3,35},{35,3},{4,36},{36... | collective-permute-start | bytes 2752520 | tf_op jit(solution)/shard_map/ppermute | solution.py:102
  139.8 3.0 %collective-permute-start.2 = (bf16[224]{0:T(256)(128)(2,1)S(1)}, bf16[224]{0:T(256)(128)(2,1)S(1)}, u32[]{:S(2)}, u32[]{:S(2)}) collective-permute-start(bf16[224]{0:T(256)(128)(2,1)S(1)} %multiply_reduce_fusion), channel_id=1, source_target_pairs={{0,32},{32,0},{1,33},{33,1},{2,34},{34,2},{3,35},{35,3},{4,36},{36... | collective-permute-start | bytes 1352 | tf_op jit(solution)/shard_map/ppermute | solution.py:103
  165.4 33.9 %copy-start.6 = (pred[224,320]{1,0:T(32,128)(4,1)S(1)}, pred[224,320]{1,0:T(32,128)(4,1)}, u32[]{:S(2)}) copy-start(pred[224,320]{1,0:T(32,128)(4,1)} %copy-done.5) | copy-start | bytes 215044
  165.5 33.9 %copy-start.8 = (pred[224,320]{1,0:T(32,128)(4,1)S(1)}, pred[224,320]{1,0:T(32,128)(4,1)}, u32[]{:S(2)}) copy-start(pred[224,320]{1,0:T(32,128)(4,1)} %copy-done.7) | copy-start | bytes 215044

commit v7 on v6

--- a/solution.py
+++ b/solution.py
@@ -89,20 +89,25 @@
     d_gate = (d_hidden * pre_up * sigmoid_gate * (1.0 + pre_gate * (1.0 - sigmoid_gate))).astype(
         jnp.bfloat16
     )
-    d_rows = jnp.dot(d_gate, gate_shard, preferred_element_type=jnp.float32) + jnp.dot(
-        d_up, up_shard, preferred_element_type=jnp.float32
-    )
-    d_rows = d_rows.astype(jnp.bfloat16)
     dp_count = group_size * shard_count
     cores = lax.axis_size("c")
-    d_view = d_rows.reshape(slots, dp_count // cores, cores, out_width)
-    keep = lax.dynamic_index_in_dim(d_view, core, axis=2, keepdims=False)
-    give = lax.dynamic_index_in_dim(d_view, 1 - core, axis=2, keepdims=False)
+    col_view = (gate_shard.shape[0], dp_count // cores, cores, out_width)
+
+    def columns(weight, which):
+        return lax.dynamic_index_in_dim(weight.reshape(col_view), which, axis=2, keepdims=False)
+
+    def part_rows(which):
+        rows = jnp.einsum(
+            "ru,ukf->krf", d_gate, columns(gate_shard, which), preferred_element_type=jnp.float32
+        ) + jnp.einsum("ru,ukf->krf", d_up, columns(up_shard, which), preferred_element_type=jnp.float32)
+        return rows.astype(jnp.bfloat16)
+
+    keep = part_rows(core)
+    give = part_rows(1 - core)
     swap = [(0, 1), (1, 0)]
     got = lax.ppermute(give, "c", perm=swap)
     inner_peer = lax.ppermute(inner, "c", perm=swap)
-    pair_sum = (keep.astype(jnp.float32) + got.astype(jnp.float32)).astype(jnp.bfloat16)
-    d_split = pair_sum.transpose(1, 0, 2)
+    d_split = (keep.astype(jnp.float32) + got.astype(jnp.float32)).astype(jnp.bfloat16)
     inner_rows = -(-slots // out_width)
     inner_both = jnp.where(core == 0, jnp.stack([inner, inner_peer]), jnp.stack([inner_peer, inner]))
     inner_block = jnp.pad(inner_both, ((0, 0), (0, inner_rows * out_width - slots)))

time: 204 us -> 199 us (0.975)
  waiting for transfers between devices: 4.13 us -> 0.32 us
    another operation x3 -> x5, local copies, waits for them, and re-layouts: 0.23 us -> 6.06 us  [the longest x2 5.83 us: columns(): weight.reshape(col_view)]
    reshape x1 -> x0, local copies, waits for them, and re-layouts: 5.48 us -> none  [shards(): d_view = d_rows.reshape(slots, dp_count // cores, cores, out_width)]
    ppermute x1, waiting for transfers between devices: 3.17 us -> 0.01 us  [shards(): other_core = lax.ppermute(same_core, 'c', perm=[(0, 1), (1, 0)])]
    unnamed x23 -> x28, local copies, waits for them, and re-layouts: 4.46 us -> 4.85 us
  transfers between devices with their start and end apart: 3 -> 3, of which waited for: 2 -> 1; matrix products, arithmetic and copies ran while one was open for 1% -> 7% of each run, Pallas kernels for 0% -> 0%
where the time goes in v7:
time: 199 us; the launch traced here: 197 us
  blocking collectives  148 us (74%)
  local copies, waits for them, and re-layouts  20.5 us (10%)
  starting transfers between devices  10.4 us (5%)
  matrix products  8.67 us (4%)
  other arithmetic  7.88 us (4%)
    all_to_all x1, blocking collectives, shards(): lax.all_to_all(payload, 'expert', split_axis=0, concat_axis=0, tiled=True)  69.6 us
    all_to_all x1, blocking collectives, shards(): lax.all_to_all(back_send, 'expert', split_axis=0, concat_axis=0, tiled=True)  32.2 us
    all_to_all x1, blocking collectives, shards(): lax.all_to_all(spread, ('sy', 'sx'), split_axis=0, concat_axis=0, tiled=T...  26 us
    all_to_all x1, blocking collectives, shards(): lax.all_to_all(ex_send, ('l', 'sy', 'sx'), split_axis=0, concat_axis=0, t...  20.1 us
    another operation x2, local copies, waits for them, and re-layouts, columns(): weight.reshape(col_view)  5.83 us
    ppermute x1, starting transfers between devices, shards(): other_core = lax.ppermute(same_core, 'c', perm=[(0, 1), (1, 0)])  5.79 us
    dynamic_slice x1, local copies, waits for them, and re-layouts, columns(): lax.dynamic_index_in_dim(weight.reshape(col_view), which, axis=2, keepdim...  5.62 us
    unnamed x28, local copies, waits for them, and re-layouts  4.85 us
  transfers between devices with their start and end apart: 3, of which 1 were waited for; matrix products, arithmetic and copies ran while one was open for 7% of the time, Pallas kernels for 0%

profile of v7, /device:TPU:1, one launch (start us, length us, event | category | flops | bytes accessed | tf_op | source)
XLA Modules:
  0.0 196.9 jit_solution(11655506835206791825)
XLA Ops:
  0.6 0.8 copy.141
  1.7 0.9 reduce-window.16
  2.9 0.9 reduce-window.14
  4.4 0.8 copy.151
  6.2 0.8 constant_dynamic-slice_fusion.3
  7.5 69.6 %all_to_all.20 = bf16[32,8,512]{2,1,0:T(8,128)(2,1)S(1)} all-to-all(bf16[32,8,512]{2,1,0:T(8,128)(2,1)S(1)} %fusion.18), channel_id=1, replica_groups=mesh['l'=2,'sy'=2,'sx'=4,'c'=2,'expert'=32] {'expert'}, dimensions={0} | all-to-all | bytes 524288 | tf_op jit(solution)/shard_map/all_to_all | solution.py:58
  78.0 26.0 %all_to_all.21 = bf16[8,224,512]{2,1,0:T(8,128)(2,1)S(1)} all-to-all(bf16[8,224,512]{2,1,0:T(8,128)(2,1)S(1)} %broadcast_in_dim.12), channel_id=1, replica_groups=mesh['l'=2,'sy'=2,'sx'=4,'c'=2,'expert'=32] {'sy','sx'}, dimensions={0} | all-to-all | bytes 3670016 | tf_op jit(solution)/shard_map/all_to_all | solution.py:64
  104.0 5.8 %collective-permute-start = (bf16[8,224,512]{2,1,0:T(8,128)(2,1)S(1)}, bf16[8,224,512]{2,1,0:T(8,128)(2,1)}, u32[]{:S(2)}, u32[]{:S(2)}) collective-permute-start(bf16[8,224,512]{2,1,0:T(8,128)(2,1)S(1)} %all_to_all.21), channel_id=1, source_target_pairs={{0,32},{32,0},{1,33},{33,1},{2,34},{34,2},{3,35},{35,3},{4,36},{36... | collective-permute-start | bytes 5505032 | tf_op jit(solution)/shard_map/ppermute | solution.py:65
  109.8 2.6 %reshape_squeeze.10 = bf16[96,16,2,128]{3,2,1,0:T(2,128)(2,1)S(1)} reshape(bf16[1,96,4096]{2,1,0:T(8,128)(2,1)} %param.12) | data formatting | bytes 1572864 | tf_op jit(solution)/shard_map/reshape;squeeze | solution.py:97
  112.4 3.3 %reshape_squeeze.4 = bf16[96,16,2,128]{3,2,1,0:T(2,128)(2,1)} reshape(bf16[1,96,4096]{2,1,0:T(8,128)(2,1)} %param.11) | data formatting | bytes 1572864 | tf_op jit(solution)/shard_map/reshape;squeeze | solution.py:97
  115.6 5.6 %constant_dynamic-slice_fusion.2 = (bf16[96,16,1,128]{3,2,1,0:T(2,128)(2,1)}, bf16[96,16,1,128]{3,2,1,0:T(2,128)(2,1)}, bf16[96,16,1,128]{3,2,1,0:T(2,128)(2,1)}, bf16[96,16,1,128]{3,2,1,0:T(2,128)(2,1)}) fusion(bf16[96,16,2,128]{3,2,1,0:T(2,128)(2,1)S(1)} %reshape_squeeze.10, s32[]{:T(128)S(6)} %select_n.103, s32[]{:T(128)S(6)} %select_n.109, ...), kind=kLoop, calls=%fused_computation.109 | loop fusion | bytes 3145736 | tf_op jit(solution)/shard_map/jit(dynamic_index_in_dim)/dynamic_slice | solution.py:97
  121.3 0.9 fusion.42
  122.3 3.2 %fusion.1 = bf16[8,2,224,512]{3,2,0,1:T(8,128)(2,1)S(1)} fusion(s32[]{:T(128)S(6)} %select_n.108, bf16[8,1,224,512]{3,2,0,1:T(8,128)(2,1)S(1)} %bitcast.110, bf16[8,1,224,512]{3,2,0,1:T(8,128)(2,1)} %bitcast.5), kind=kLoop, calls=%fused_computation.5 | loop fusion | flops 3670016 | bytes 7340036 | tf_op jit(solution)/shard_map/stack | solution.py:66
  126.4 0.9 copy-done.1
  127.3 0.7 fusion.6
  128.0 0.7 fusion.4
  128.9 0.7 fusion.23
  130.9 1.4 fusion.3
  132.3 2.1 %collective-permute-start.1 = (bf16[16,224,128]{2,1,0:T(8,128)(2,1)}, bf16[16,224,128]{2,1,0:T(8,128)(2,1)}, u32[]{:S(2)}, u32[]{:S(2)}) collective-permute-start(bf16[16,224,128]{2,1,0:T(8,128)(2,1)} %fusion.3), channel_id=1, source_target_pairs={{0,32},{32,0},{1,33},{33,1},{2,34},{34,2},{3,35},{35,3},{4,36},{36... | collective-permute-start | bytes 2752520 | tf_op jit(solution)/shard_map/ppermute | solution.py:108
  135.7 2.5 %collective-permute-start.2 = (bf16[224]{0:T(256)(128)(2,1)S(1)}, bf16[224]{0:T(256)(128)(2,1)S(1)}, u32[]{:S(2)}, u32[]{:S(2)}) collective-permute-start(bf16[224]{0:T(256)(128)(2,1)S(1)} %multiply_reduce_fusion), channel_id=1, source_target_pairs={{0,32},{32,0},{1,33},{33,1},{2,34},{34,2},{3,35},{35,3},{4,36},{36... | collective-permute-start | bytes 1352 | tf_op jit(solution)/shard_map/ppermute | solution.py:109
  139.1 1.7 fusion.2
  140.9 20.1 %all_to_all.22 = bf16[16,240,128]{2,1,0:T(8,128)(2,1)S(1)} all-to-all(bf16[16,240,128]{2,1,0:T(8,128)(2,1)S(1)} %pad_maximum_fusion), channel_id=1, replica_groups=mesh['l'=2,'sy'=2,'sx'=4,'c'=2,'expert'=32] {'l','sy','sx'}, dimensions={0} | all-to-all | bytes 1966080 | tf_op jit(solution)/shard_map/all_to_all | solution.py:121
  161.8 32.2 %all_to_all.23 = bf16[32,2,8,128]{3,1,2,0:T(2,128)(2,1)S(1)} all-to-all(bf16[32,2,8,128]{3,1,2,0:T(2,128)(2,1)S(1)} %fusion.21), channel_id=1, replica_groups=mesh['l'=2,'sy'=2,'sx'=4,'c'=2,'expert'=32] {'expert'}, dimensions={0} | all-to-all | bytes 262144 | tf_op jit(solution)/shard_map/all_to_all | solution.py:136
  194.2 0.8 convolution_convert_fusion.2
  (101 shorter events, 10.7 us)
Async XLA Ops:
  0.6 128.3 %copy-start = (bf16[1,96,4096]{2,1,0:T(8,128)(2,1)S(1)}, bf16[1,96,4096]{2,1,0:T(8,128)(2,1)}, u32[]{:S(2)}) copy-start(bf16[1,96,4096]{2,1,0:T(8,128)(2,1)} %param.13) | copy-start | bytes 2359300
  5.3 1.6 copy-start.8
  5.4 1.6 copy-start.10
  77.1 0.7 copy-start.7
  104.0 18.3 %collective-permute-start = (bf16[8,224,512]{2,1,0:T(8,128)(2,1)S(1)}, bf16[8,224,512]{2,1,0:T(8,128)(2,1)}, u32[]{:S(2)}, u32[]{:S(2)}) collective-permute-start(bf16[8,224,512]{2,1,0:T(8,128)(2,1)S(1)} %all_to_all.21), channel_id=1, source_target_pairs={{0,32},{32,0},{1,33},{33,1},{2,34},{34,2},{3,35},{35,3},{4,36},{36... | collective-permute-start | bytes 5505032 | tf_op jit(solution)/shard_map/ppermute | solution.py:65
  126.1 1.1 copy-start.1
  126.4 1.6 copy-start.2
  128.9 1.1 copy-start.5
  129.7 1.2 copy-start.3
  132.3 6.8 %collective-permute-start.1 = (bf16[16,224,128]{2,1,0:T(8,128)(2,1)}, bf16[16,224,128]{2,1,0:T(8,128)(2,1)}, u32[]{:S(2)}, u32[]{:S(2)}) collective-permute-start(bf16[16,224,128]{2,1,0:T(8,128)(2,1)} %fusion.3), channel_id=1, source_target_pairs={{0,32},{32,0},{1,33},{33,1},{2,34},{34,2},{3,35},{35,3},{4,36},{36... | collective-permute-start | bytes 2752520 | tf_op jit(solution)/shard_map/ppermute | solution.py:108
  135.1 3.1 %copy-start.4 = (bf16[96,16,1,128]{3,2,1,0:T(2,128)(2,1)S(1)}, bf16[96,16,1,128]{3,2,1,0:T(2,128)(2,1)}, u32[]{:S(2)}) copy-start(bf16[96,16,1,128]{3,2,1,0:T(2,128)(2,1)} %get-tuple-element.41) | copy-start | bytes 1179652
  135.7 3.4 %copy-start.6 = (bf16[96,16,1,128]{3,2,1,0:T(2,128)(2,1)S(1)}, bf16[96,16,1,128]{3,2,1,0:T(2,128)(2,1)}, u32[]{:S(2)}) copy-start(bf16[96,16,1,128]{3,2,1,0:T(2,128)(2,1)} %get-tuple-element.20) | copy-start | bytes 1179652
  135.7 3.3 %collective-permute-start.2 = (bf16[224]{0:T(256)(128)(2,1)S(1)}, bf16[224]{0:T(256)(128)(2,1)S(1)}, u32[]{:S(2)}, u32[]{:S(2)}) collective-permute-start(bf16[224]{0:T(256)(128)(2,1)S(1)} %multiply_reduce_fusion), channel_id=1, source_target_pairs={{0,32},{32,0},{1,33},{33,1},{2,34},{34,2},{3,35},{35,3},{4,36},{36... | collective-permute-start | bytes 1352 | tf_op jit(solution)/shard_map/ppermute | solution.py:109
  161.1 34.3 %copy-start.9 = (pred[224,320]{1,0:T(32,128)(4,1)S(1)}, pred[224,320]{1,0:T(32,128)(4,1)}, u32[]{:S(2)}) copy-start(pred[224,320]{1,0:T(32,128)(4,1)} %copy-done.8) | copy-start | bytes 215044
  161.1 34.3 %copy-start.11 = (pred[224,320]{1,0:T(32,128)(4,1)S(1)}, pred[224,320]{1,0:T(32,128)(4,1)}, u32[]{:S(2)}) copy-start(pred[224,320]{1,0:T(32,128)(4,1)} %copy-done.10) | copy-start | bytes 215044

commit v8 on v5

--- a/solution.py
+++ b/solution.py
@@ -78,13 +78,9 @@
     sigmoid_gate = jax.nn.sigmoid(pre_gate)
     activated = pre_gate * sigmoid_gate
     hidden = (activated * pre_up).astype(jnp.bfloat16)
-    outputs = jnp.dot(hidden, down_shard, preferred_element_type=jnp.float32).astype(jnp.bfloat16)
-    outputs = lax.optimization_barrier(outputs)
-    inner = jnp.sum(
-        rows_cot.astype(jnp.float32) * outputs.astype(jnp.float32), axis=1
-    ).astype(jnp.bfloat16)
-    d_hidden = lax.dot_general(rows_cot, down_shard, contract_model, preferred_element_type=jnp.float32)
-    d_hidden = d_hidden * probs_in.reshape(-1, 1)
+    d_down = lax.dot_general(rows_cot, down_shard, contract_model, preferred_element_type=jnp.float32)
+    inner = jnp.sum(hidden.astype(jnp.float32) * d_down, axis=1).astype(jnp.bfloat16)
+    d_hidden = d_down * probs_in.reshape(-1, 1)
     d_up = (d_hidden * activated).astype(jnp.bfloat16)
     d_gate = (d_hidden * pre_up * sigmoid_gate * (1.0 + pre_gate * (1.0 - sigmoid_gate))).astype(
         jnp.bfloat16

time: 193 us -> 192 us (level)
  no operation moved by 1% of the time
where the time goes in v8:
time: 192 us
  blocking collectives  162 us (84%)
  local copies, waits for them, and re-layouts  8.21 us (4%)
  other arithmetic  6.43 us (3%)
  starting transfers between devices  5.77 us (3%)
  matrix products  5.34 us (3%)
  waiting for transfers between devices  3.35 us (2%)
    all_to_all x1, blocking collectives, shards(): lax.all_to_all(payload, 'expert', split_axis=0, concat_axis=0, tiled=True)  69.6 us
    all_to_all x1, blocking collectives, shards(): lax.all_to_all(back_send, 'expert', split_axis=0, concat_axis=0, tiled=True)  33.8 us
    all_to_all x1, blocking collectives, shards(): lax.all_to_all(ex_send, ('l', 'sy', 'sx', 'c'), split_axis=0, concat_axis...  32.1 us
    all_to_all x1, blocking collectives, shards(): lax.all_to_all(spread, ('sy', 'sx'), split_axis=0, concat_axis=0, tiled=T...  26 us
    ppermute x1, starting transfers between devices, shards(): other_core = lax.ppermute(same_core, 'c', perm=[(0, 1), (1, 0)])  5.77 us
    unnamed x12, local copies, waits for them, and re-layouts  4.04 us
  transfers between devices with their start and end apart: 1, of which 1 were waited for; matrix products, arithmetic and copies ran while one was open for 0% of the time, Pallas kernels for 0%

profile of v8, /device:TPU:1, one launch (start us, length us, event | category | flops | bytes accessed | tf_op | source)
XLA Modules:
  0.0 191.7 jit_solution(6864334719799648407)
XLA Ops:
  0.6 0.8 copy.103
  1.7 0.9 reduce-window.16
  2.9 0.9 reduce-window.14
  4.4 0.8 copy.112
  6.2 0.8 constant_dynamic-slice_fusion
  6.9 0.3 convolution_convert_fusion
  7.5 69.6 %all_to_all.20 = bf16[32,8,512]{2,1,0:T(8,128)(2,1)S(1)} all-to-all(bf16[32,8,512]{2,1,0:T(8,128)(2,1)S(1)} %fusion.19), channel_id=1, replica_groups=mesh['l'=2,'sy'=2,'sx'=4,'c'=2,'expert'=32] {'expert'}, dimensions={0} | all-to-all | bytes 524288 | tf_op jit(solution)/shard_map/all_to_all | solution.py:58
  77.3 26.0 %all_to_all.21 = bf16[8,224,512]{2,1,0:T(8,128)(2,1)S(1)} all-to-all(bf16[8,224,512]{2,1,0:T(8,128)(2,1)S(1)} %broadcast_in_dim.12), channel_id=1, replica_groups=mesh['l'=2,'sy'=2,'sx'=4,'c'=2,'expert'=32] {'sy','sx'}, dimensions={0} | all-to-all | bytes 3670016 | tf_op jit(solution)/shard_map/all_to_all | solution.py:64
  103.4 5.8 %collective-permute-start = (bf16[8,224,512]{2,1,0:T(8,128)(2,1)S(1)}, bf16[8,224,512]{2,1,0:T(8,128)(2,1)}, u32[]{:S(2)}, u32[]{:S(2)}) collective-permute-start(bf16[8,224,512]{2,1,0:T(8,128)(2,1)S(1)} %all_to_all.21), channel_id=1, source_target_pairs={{0,32},{32,0},{1,33},{33,1},{2,34},{34,2},{3,35},{35,3},{4,36},{36... | collective-permute-start | bytes 5505032 | tf_op jit(solution)/shard_map/ppermute | solution.py:65
  109.3 3.4 %collective-permute-done = bf16[8,224,512]{2,1,0:T(8,128)(2,1)} collective-permute-done((bf16[8,224,512]{2,1,0:T(8,128)(2,1)S(1)}, bf16[8,224,512]{2,1,0:T(8,128)(2,1)}, u32[]{:S(2)}, u32[]{:S(2)}) %collective-permute-start) | collective-permute-done | bytes 1835040 | tf_op jit(solution)/shard_map/ppermute | solution.py:65
  112.7 3.1 %fusion.2 = bf16[8,2,224,512]{3,2,1,0:T(8,128)(2,1)S(1)} fusion(s32[]{:T(128)S(6)} %select_n.90, bf16[8,1,224,512]{3,2,1,0:T(8,128)(2,1)S(1)} %bitcast.102, bf16[8,1,224,512]{3,2,1,0:T(8,128)(2,1)} %bitcast.5), kind=kLoop, calls=%fused_computation.7 | loop fusion | flops 3670016 | bytes 7340036 | tf_op jit(solution)/shard_map/stack | solution.py:66
  115.8 0.4 slice_bitcast_fusion
  116.5 0.7 fusion.6
  117.2 0.4 copy-done.1
  117.6 0.7 fusion.9
  118.6 0.9 copy-done.2
  119.5 0.7 multiply_reduce_fusion
  120.2 0.7 fusion.4
  120.9 0.7 fusion.3
  121.6 0.3 copy.140
  122.1 32.1 %all_to_all.22 = bf16[32,240,128]{2,1,0:T(8,128)(2,1)S(1)} all-to-all(bf16[32,240,128]{2,1,0:T(8,128)(2,1)S(1)} %pad_maximum_fusion), channel_id=1, replica_groups=mesh['l'=2,'sy'=2,'sx'=4,'c'=2,'expert'=32] {'l','sy','sx','c'}, dimensions={0} | all-to-all | bytes 3932160 | tf_op jit(solution)/shard_map/all_to_all | solution.py:102
  155.0 33.8 %all_to_all.23 = bf16[32,2,8,128]{3,1,2,0:T(2,128)(2,1)S(1)} all-to-all(bf16[32,2,8,128]{3,1,2,0:T(2,128)(2,1)S(1)} %fusion.22), channel_id=1, replica_groups=mesh['l'=2,'sy'=2,'sx'=4,'c'=2,'expert'=32] {'expert'}, dimensions={0} | all-to-all | bytes 262144 | tf_op jit(solution)/shard_map/all_to_all | solution.py:114
  190.1 0.8 convolution_convert_fusion.1
  191.0 0.7 copy.125
  (67 shorter events, 5.3 us)
Async XLA Ops:
  0.6 115.9 %copy-start = (bf16[1,96,4096]{2,1,0:T(8,128)(2,1)S(1)}, bf16[1,96,4096]{2,1,0:T(8,128)(2,1)}, u32[]{:S(2)}) copy-start(bf16[1,96,4096]{2,1,0:T(8,128)(2,1)} %param.11) | copy-start | bytes 2359300
  103.4 9.3 %collective-permute-start = (bf16[8,224,512]{2,1,0:T(8,128)(2,1)S(1)}, bf16[8,224,512]{2,1,0:T(8,128)(2,1)}, u32[]{:S(2)}, u32[]{:S(2)}) collective-permute-start(bf16[8,224,512]{2,1,0:T(8,128)(2,1)S(1)} %all_to_all.21), channel_id=1, source_target_pairs={{0,32},{32,0},{1,33},{33,1},{2,34},{34,2},{3,35},{35,3},{4,36},{36... | collective-permute-start | bytes 5505032 | tf_op jit(solution)/shard_map/ppermute | solution.py:65
  116.5 1.1 copy-start.1
  118.3 1.1 copy-start.2

commit v9 on v5

--- a/solution.py
+++ b/solution.py
@@ -49,15 +49,19 @@
     cot_chunk = lax.dynamic_slice_in_dim(cotangent, part * chunk, chunk, axis=1)
     both_chunk = jnp.concatenate([tok_chunk, cot_chunk], axis=1)
     rows_sent = jnp.dot(by_token, both_chunk, preferred_element_type=jnp.float32).astype(jnp.bfloat16)
-    rows_sent = rows_sent.reshape(dest_count, send_rows, 2 * chunk)
+    row_words = send_rows * 2 * chunk
+    rows_sent = rows_sent.reshape(dest_count, row_words)
     probs_sent = jnp.dot(
         placing, gate_probs.reshape(-1), preferred_element_type=jnp.float32
     ).astype(jnp.bfloat16)
-    probs_row = jnp.pad(probs_sent.reshape(dest_count, 1, send_rows), ((0, 0), (0, 0), (0, 2 * chunk - send_rows)))
-    payload = jnp.concatenate([rows_sent, probs_row], axis=1)
+    fwd_pad = (-(row_words + send_rows)) % 128
+    payload = jnp.concatenate(
+        [rows_sent, probs_sent.reshape(dest_count, send_rows), jnp.zeros((dest_count, fwd_pad), jnp.bfloat16)],
+        axis=1,
+    )
     recv = lax.all_to_all(payload, "expert", split_axis=0, concat_axis=0, tiled=True)
-    probs_in = recv[:, send_rows, :send_rows].reshape(slots).astype(jnp.float32)
-    rows_in = recv[:, :send_rows, :].reshape(slots, 2 * chunk)
+    probs_in = recv[:, row_words:row_words + send_rows].reshape(slots).astype(jnp.float32)
+    rows_in = recv[:, :row_words].reshape(slots, 2 * chunk)
 
     chips = lax.axis_size("sy") * lax.axis_size("sx")
     spread = jnp.broadcast_to(rows_in[None], (chips,) + rows_in.shape)
@@ -112,16 +116,21 @@
     inner_sum = inner_sum[:, :slots].reshape(group_size, dest_count, send_rows).transpose(1, 0, 2)
     inner_hi = inner_sum.astype(jnp.bfloat16)
     inner_lo = (inner_sum - inner_hi.astype(jnp.float32)).astype(jnp.bfloat16)
-    inner_pair = jnp.concatenate([inner_hi, inner_lo], axis=2).reshape(dest_count, group_size, 1, 2 * send_rows)
-    inner_pair = jnp.pad(inner_pair, ((0, 0), (0, 0), (0, 0), (0, out_width - 2 * send_rows)))
-    back_send = jnp.concatenate([grads_chunk, inner_pair], axis=2)
+    grad_words = group_size * send_rows * out_width
+    inner_pair = jnp.stack([inner_hi, inner_lo], axis=1).reshape(dest_count, 2 * group_size * send_rows)
+    back_pad = (-(grad_words + 2 * group_size * send_rows)) % 128
+    back_send = jnp.concatenate(
+        [grads_chunk.reshape(dest_count, grad_words), inner_pair, jnp.zeros((dest_count, back_pad), jnp.bfloat16)],
+        axis=1,
+    )
     back = lax.all_to_all(back_send, "expert", split_axis=0, concat_axis=0, tiled=True)
 
-    back = back.transpose(1, 0, 2, 3)
-    grads_back = back[:, :, :send_rows, :].reshape(group_size * slots, out_width)
-    inner_back = back[:, :, send_rows, :2 * send_rows]
-    inner_hi = inner_back[:, :, :send_rows].reshape(group_size * slots)
-    inner_lo = inner_back[:, :, send_rows:].reshape(group_size * slots)
+    grads_back = back[:, :grad_words].reshape(dest_count, group_size, send_rows, out_width)
+    grads_back = grads_back.transpose(1, 0, 2, 3).reshape(group_size * slots, out_width)
+    inner_back = back[:, grad_words:grad_words + 2 * group_size * send_rows]
+    inner_back = inner_back.reshape(dest_count, 2, group_size, send_rows).transpose(1, 2, 0, 3)
+    inner_hi = inner_back[0].reshape(group_size * slots)
+    inner_lo = inner_back[1].reshape(group_size * slots)
     contract_rows = (((0,), (0,)), ((), ()))
     d_tokens = lax.dot_general(
         by_token_all, grads_back, contract_rows, preferred_element_type=jnp.float32

time: 193 us -> 196 us (1.016)
  local copies, waits for them, and re-layouts: 7.96 us -> 10.3 us
  blocking collectives: 162 us -> 160 us
    unnamed x12 -> x18, local copies, waits for them, and re-layouts: 3.48 us -> 4.47 us
where the time goes in v9:
time: 196 us; the launch traced here: 195 us
  blocking collectives  160 us (82%)
  local copies, waits for them, and re-layouts  10.3 us (5%)
  other arithmetic  8.22 us (4%)
  matrix products  6 us (3%)
  starting transfers between devices  5.5 us (3%)
  waiting for transfers between devices  3.41 us (2%)
    all_to_all x1, blocking collectives, shards(): lax.all_to_all(payload, 'expert', split_axis=0, concat_axis=0, tiled=True)  68.4 us
    all_to_all x1, blocking collectives, shards(): lax.all_to_all(back_send, 'expert', split_axis=0, concat_axis=0, tiled=True)  33.5 us
    all_to_all x1, blocking collectives, shards(): lax.all_to_all(ex_send, ('l', 'sy', 'sx', 'c'), split_axis=0, concat_axis...  32.1 us
    all_to_all x1, blocking collectives, shards(): lax.all_to_all(spread, ('sy', 'sx'), split_axis=0, concat_axis=0, tiled=T...  26.3 us
    ppermute x1, starting transfers between devices, shards(): other_core = lax.ppermute(same_core, 'c', perm=[(0, 1), (1, 0)])  5.5 us
    unnamed x18, local copies, waits for them, and re-layouts  4.47 us
  transfers between devices with their start and end apart: 1, of which 1 were waited for; matrix products, arithmetic and copies ran while one was open for 0% of the time, Pallas kernels for 0%

profile of v9, /device:TPU:1, one launch (start us, length us, event | category | flops | bytes accessed | tf_op | source)
XLA Modules:
  0.0 194.9 jit_solution(475419971000132966)
XLA Ops:
  0.6 0.8 copy.149
  1.7 0.9 reduce-window.16
  2.9 0.9 reduce-window.14
  4.4 0.8 copy.158
  6.2 0.8 constant_dynamic-slice_fusion
  8.2 0.7 reduce.10
  9.1 68.4 %all_to_all.34 = bf16[32,2,1856]{2,1,0:T(2,128)(2,1)S(1)} all-to-all(bf16[32,2,1856]{2,1,0:T(2,128)(2,1)S(1)} %reshape.283), channel_id=1, replica_groups=mesh['l'=2,'sy'=2,'sx'=4,'c'=2,'expert'=32] {'expert'}, dimensions={0} | all-to-all | bytes 475136 | tf_op jit(solution)/shard_map/all_to_all | solution.py:62
  78.4 26.3 %all_to_all.35 = bf16[8,224,512]{2,1,0:T(8,128)(2,1)S(1)} all-to-all(bf16[8,224,512]{2,1,0:T(8,128)(2,1)S(1)} %broadcast_in_dim.32), channel_id=1, replica_groups=mesh['l'=2,'sy'=2,'sx'=4,'c'=2,'expert'=32] {'sy','sx'}, dimensions={0} | all-to-all | bytes 3670016 | tf_op jit(solution)/shard_map/all_to_all | solution.py:68
  104.7 5.5 %collective-permute-start = (bf16[8,224,512]{2,1,0:T(8,128)(2,1)S(1)}, bf16[8,224,512]{2,1,0:T(8,128)(2,1)}, u32[]{:S(2)}, u32[]{:S(2)}) collective-permute-start(bf16[8,224,512]{2,1,0:T(8,128)(2,1)S(1)} %all_to_all.35), channel_id=1, source_target_pairs={{0,32},{32,0},{1,33},{33,1},{2,34},{34,2},{3,35},{35,3},{4,36},{36... | collective-permute-start | bytes 5505032 | tf_op jit(solution)/shard_map/ppermute | solution.py:69
  110.3 3.4 %collective-permute-done = bf16[8,224,512]{2,1,0:T(8,128)(2,1)} collective-permute-done((bf16[8,224,512]{2,1,0:T(8,128)(2,1)S(1)}, bf16[8,224,512]{2,1,0:T(8,128)(2,1)}, u32[]{:S(2)}, u32[]{:S(2)}) %collective-permute-start) | collective-permute-done | bytes 1835040 | tf_op jit(solution)/shard_map/ppermute | solution.py:69
  113.7 3.2 %fusion.2 = bf16[8,2,224,512]{3,2,0,1:T(8,128)(2,1)S(1)} fusion(s32[]{:T(128)S(6)} %select_n.90, bf16[8,1,224,512]{3,2,0,1:T(8,128)(2,1)S(1)} %bitcast.123, bf16[8,1,224,512]{3,2,0,1:T(8,128)(2,1)} %bitcast.5), kind=kLoop, calls=%fused_computation.8 | loop fusion | flops 3670016 | bytes 7340036 | tf_op jit(solution)/shard_map/stack | solution.py:70
  118.0 0.9 copy-done.1
  118.9 0.7 fusion.6
  119.6 0.7 fusion.9
  120.4 0.7 convolution_convert_fusion
  121.0 0.7 convolution_multiply_fusion
  121.8 0.6 multiply_reduce_fusion
  122.3 0.7 fusion.4
  123.0 0.7 fusion.3
  124.2 32.1 %all_to_all.36 = bf16[32,240,128]{2,1,0:T(8,128)(2,1)S(1)} all-to-all(bf16[32,240,128]{2,1,0:T(8,128)(2,1)S(1)} %pad_maximum_fusion), channel_id=1, replica_groups=mesh['l'=2,'sy'=2,'sx'=4,'c'=2,'expert'=32] {'l','sy','sx','c'}, dimensions={0} | all-to-all | bytes 3932160 | tf_op jit(solution)/shard_map/all_to_all | solution.py:110
  157.3 0.7 reduce.11
  158.2 33.5 %all_to_all.37 = bf16[32,2,960]{2,1,0:T(2,128)(2,1)S(1)} all-to-all(bf16[32,2,960]{2,1,0:T(2,128)(2,1)S(1)} %reshape.285), channel_id=1, replica_groups=mesh['l'=2,'sy'=2,'sx'=4,'c'=2,'expert'=32] {'expert'}, dimensions={0} | all-to-all | bytes 245760 | tf_op jit(solution)/shard_map/all_to_all | solution.py:126
  193.3 0.8 convolution_convert_fusion.2
  194.2 0.7 copy.173
  (88 shorter events, 8.7 us)
Async XLA Ops:
  0.6 119.7 %copy-start = (bf16[1,96,4096]{2,1,0:T(8,128)(2,1)S(1)}, bf16[1,96,4096]{2,1,0:T(8,128)(2,1)}, u32[]{:S(2)}) copy-start(bf16[1,96,4096]{2,1,0:T(8,128)(2,1)} %param.13) | copy-start | bytes 2359300
  104.7 9.0 %collective-permute-start = (bf16[8,224,512]{2,1,0:T(8,128)(2,1)S(1)}, bf16[8,224,512]{2,1,0:T(8,128)(2,1)}, u32[]{:S(2)}, u32[]{:S(2)}) collective-permute-start(bf16[8,224,512]{2,1,0:T(8,128)(2,1)S(1)} %all_to_all.35), channel_id=1, source_target_pairs={{0,32},{32,0},{1,33},{33,1},{2,34},{34,2},{3,35},{35,3},{4,36},{36... | collective-permute-start | bytes 5505032 | tf_op jit(solution)/shard_map/ppermute | solution.py:69
  117.8 1.1 copy-start.1
  118.0 1.6 copy-start.2

commit v10 on v5

--- a/solution.py
+++ b/solution.py
@@ -67,23 +67,26 @@
     gathered = lax.dynamic_slice_in_dim(by_core, core, 2, axis=1).reshape((shard_count,) + rows_in.shape)
     tok_parts = gathered[:, :, :chunk]
     cot_parts = gathered[:, :, chunk:]
-    rows_tok = tok_parts.transpose(1, 0, 2).reshape(slots, model_width)
-    rows_cot = cot_parts.transpose(1, 0, 2).reshape(slots, model_width)
     gate_shard = w_gate[0]
     up_shard = w_up[0]
     down_shard = w_down[0]
-    contract_model = (((1,), (1,)), ((), ()))
-    pre_gate = lax.dot_general(rows_tok, gate_shard, contract_model, preferred_element_type=jnp.float32)
-    pre_up = lax.dot_general(rows_tok, up_shard, contract_model, preferred_element_type=jnp.float32)
+    contract_parts = (((0, 2), (1, 2)), ((), ()))
+
+    def by_parts(weight):
+        return weight.reshape(weight.shape[0], shard_count, chunk)
+
+    pre_gate = lax.dot_general(tok_parts, by_parts(gate_shard), contract_parts, preferred_element_type=jnp.float32)
+    pre_up = lax.dot_general(tok_parts, by_parts(up_shard), contract_parts, preferred_element_type=jnp.float32)
     sigmoid_gate = jax.nn.sigmoid(pre_gate)
     activated = pre_gate * sigmoid_gate
     hidden = (activated * pre_up).astype(jnp.bfloat16)
     outputs = jnp.dot(hidden, down_shard, preferred_element_type=jnp.float32).astype(jnp.bfloat16)
     outputs = lax.optimization_barrier(outputs)
+    out_parts = outputs.reshape(slots, shard_count, chunk).transpose(1, 0, 2)
     inner = jnp.sum(
-        rows_cot.astype(jnp.float32) * outputs.astype(jnp.float32), axis=1
+        cot_parts.astype(jnp.float32) * out_parts.astype(jnp.float32), axis=(0, 2)
     ).astype(jnp.bfloat16)
-    d_hidden = lax.dot_general(rows_cot, down_shard, contract_model, preferred_element_type=jnp.float32)
+    d_hidden = lax.dot_general(cot_parts, by_parts(down_shard), contract_parts, preferred_element_type=jnp.float32)
     d_hidden = d_hidden * probs_in.reshape(-1, 1)
     d_up = (d_hidden * activated).astype(jnp.bfloat16)
     d_gate = (d_hidden * pre_up * sigmoid_gate * (1.0 + pre_gate * (1.0 - sigmoid_gate))).astype(

time: 193 us -> 194 us (level)
  waiting for transfers between devices: 3.35 us -> 0.01 us
  local copies, waits for them, and re-layouts: 7.96 us -> 10.5 us
    ppermute x1, waiting for transfers between devices: 3.35 us -> 0.01 us  [shards(): other_core = lax.ppermute(same_core, 'c', perm=[(0, 1), (1, 0)])]
    unnamed x12 -> x28, local copies, waits for them, and re-layouts: 3.48 us -> 6.8 us
  transfers between devices with their start and end apart: 1 -> 1, of which waited for: 1 -> 0; matrix products, arithmetic and copies ran while one was open for 0% -> 2% of each run, Pallas kernels for 0% -> 0%
where the time goes in v10:
time: 194 us; the launch traced here: 193 us
  blocking collectives  162 us (84%)
  local copies, waits for them, and re-layouts  10.5 us (5%)
  other arithmetic  8.27 us (4%)
  matrix products  5.97 us (3%)
  starting transfers between devices  5.79 us (3%)
    all_to_all x1, blocking collectives, shards(): lax.all_to_all(payload, 'expert', split_axis=0, concat_axis=0, tiled=True)  69.7 us
    all_to_all x1, blocking collectives, shards(): lax.all_to_all(back_send, 'expert', split_axis=0, concat_axis=0, tiled=True)  33.8 us
    all_to_all x1, blocking collectives, shards(): lax.all_to_all(ex_send, ('l', 'sy', 'sx', 'c'), split_axis=0, concat_axis...  31.9 us
    all_to_all x1, blocking collectives, shards(): lax.all_to_all(spread, ('sy', 'sx'), split_axis=0, concat_axis=0, tiled=T...  26.2 us
    unnamed x28, local copies, waits for them, and re-layouts  6.8 us
    ppermute x1, starting transfers between devices, shards(): other_core = lax.ppermute(same_core, 'c', perm=[(0, 1), (1, 0)])  5.79 us
  transfers between devices with their start and end apart: 1, of which 0 were waited for; matrix products, arithmetic and copies ran while one was open for 2% of the time, Pallas kernels for 0%

profile of v10, /device:TPU:1, one launch (start us, length us, event | category | flops | bytes accessed | tf_op | source)
XLA Modules:
  0.0 193.3 jit_solution(15083601080986346502)
XLA Ops:
  0.6 0.8 copy.115
  1.6 0.9 reduce-window.16
  2.8 0.9 reduce-window.14
  4.3 0.8 copy.124
  6.1 0.8 constant_dynamic-slice_fusion
  7.4 69.7 %all_to_all.20 = bf16[32,8,512]{2,1,0:T(8,128)(2,1)S(1)} all-to-all(bf16[32,8,512]{2,1,0:T(8,128)(2,1)S(1)} %fusion.37), channel_id=1, replica_groups=mesh['l'=2,'sy'=2,'sx'=4,'c'=2,'expert'=32] {'expert'}, dimensions={0} | all-to-all | bytes 524288 | tf_op jit(solution)/shard_map/all_to_all | solution.py:58
  77.1 0.7 copy-done.4
  78.1 26.2 %all_to_all.21 = bf16[8,224,512]{2,1,0:T(8,128)(2,1)S(1)} all-to-all(bf16[8,224,512]{2,1,0:T(8,128)(2,1)S(1)} %broadcast_in_dim.12), channel_id=1, replica_groups=mesh['l'=2,'sy'=2,'sx'=4,'c'=2,'expert'=32] {'sy','sx'}, dimensions={0} | all-to-all | bytes 3670016 | tf_op jit(solution)/shard_map/all_to_all | solution.py:64
  104.2 5.8 %collective-permute-start = (bf16[8,224,512]{2,1,0:T(8,128)(2,1)S(1)}, bf16[8,224,512]{2,1,0:T(8,128)(2,1)}, u32[]{:S(2)}, u32[]{:S(2)}) collective-permute-start(bf16[8,224,512]{2,1,0:T(8,128)(2,1)S(1)} %all_to_all.21), channel_id=1, source_target_pairs={{0,32},{32,0},{1,33},{33,1},{2,34},{34,2},{3,35},{35,3},{4,36},{36... | collective-permute-start | bytes 5505032 | tf_op jit(solution)/shard_map/ppermute | solution.py:65
  110.1 1.1 copy.147
  111.1 1.1 copy.148
  112.2 1.1 copy.146
  113.3 0.9 fusion.60
  114.3 3.2 %fusion.2 = bf16[8,2,224,512]{3,2,1,0:T(8,128)(2,1)S(1)} fusion(s32[]{:T(128)S(6)} %select_n.90, bf16[8,1,224,512]{3,2,1,0:T(8,128)(2,1)S(1)} %bitcast.116, bf16[8,1,224,512]{3,2,1,0:T(8,128)(2,1)} %bitcast.5), kind=kLoop, calls=%fused_computation.8 | loop fusion | flops 3670016 | bytes 7340036 | tf_op jit(solution)/shard_map/stack | solution.py:66
  117.6 0.7 fusion.15
  118.3 0.7 fusion.18
  119.0 0.7 convolution_convert_fusion
  121.2 0.7 fusion.21
  121.9 0.7 fusion.26
  122.6 0.7 fusion.11
  123.8 31.9 %all_to_all.22 = bf16[32,240,128]{2,1,0:T(8,128)(2,1)S(1)} all-to-all(bf16[32,240,128]{2,1,0:T(8,128)(2,1)S(1)} %pad_maximum_fusion), channel_id=1, replica_groups=mesh['l'=2,'sy'=2,'sx'=4,'c'=2,'expert'=32] {'l','sy','sx','c'}, dimensions={0} | all-to-all | bytes 3932160 | tf_op jit(solution)/shard_map/all_to_all | solution.py:109
  156.6 33.8 %all_to_all.23 = bf16[32,2,8,128]{3,1,2,0:T(2,128)(2,1)S(1)} all-to-all(bf16[32,2,8,128]{3,1,2,0:T(2,128)(2,1)S(1)} %fusion.40), channel_id=1, replica_groups=mesh['l'=2,'sy'=2,'sx'=4,'c'=2,'expert'=32] {'expert'}, dimensions={0} | all-to-all | bytes 262144 | tf_op jit(solution)/shard_map/all_to_all | solution.py:121
  190.6 0.8 convolution_convert_fusion.2
  192.6 0.7 copy.139
  (84 shorter events, 7.1 us)
Async XLA Ops:
  5.3 1.6 copy-start.8
  7.3 102.8 %copy-start.1 = (bf16[1,96,4096]{2,1,0:T(8,128)(2,1)S(1)}, bf16[1,96,4096]{2,1,0:T(8,128)(2,1)}, u32[]{:S(2)}) copy-start(bf16[1,96,4096]{2,1,0:T(8,128)(2,1)} %param.12) | copy-start | bytes 2359300
  77.1 0.7 copy-start.4
  77.9 33.2 %copy-start = (bf16[1,96,4096]{2,1,0:T(8,128)(2,1)S(1)}, bf16[1,96,4096]{2,1,0:T(8,128)(2,1)}, u32[]{:S(2)}) copy-start(bf16[1,96,4096]{2,1,0:T(8,128)(2,1)} %param.11) | copy-start | bytes 2359300
  104.2 10.0 %collective-permute-start = (bf16[8,224,512]{2,1,0:T(8,128)(2,1)S(1)}, bf16[8,224,512]{2,1,0:T(8,128)(2,1)}, u32[]{:S(2)}, u32[]{:S(2)}) collective-permute-start(bf16[8,224,512]{2,1,0:T(8,128)(2,1)S(1)} %all_to_all.21), channel_id=1, source_target_pairs={{0,32},{32,0},{1,33},{33,1},{2,34},{34,2},{3,35},{35,3},{4,36},{36... | collective-permute-start | bytes 5505032 | tf_op jit(solution)/shard_map/ppermute | solution.py:65
  110.0 2.2 %copy-start.2 = (bf16[1,96,4096]{2,1,0:T(8,128)(2,1)S(1)}, bf16[1,96,4096]{2,1,0:T(8,128)(2,1)}, u32[]{:S(2)}) copy-start(bf16[1,96,4096]{2,1,0:T(8,128)(2,1)} %param.13) | copy-start | bytes 2359300
  114.3 3.3 %copy-start.7 = (bf16[12,8,16,256]{3,2,1,0:T(8,128)(2,1)S(1)}, bf16[12,8,16,256]{3,2,1,0:T(8,128)(2,1)}, u32[]{:S(2)}) copy-start(bf16[12,8,16,256]{3,2,1,0:T(8,128)(2,1)} %copy.147) | copy-start | bytes 2359300
  114.3 4.0 %copy-start.6 = (bf16[12,8,16,256]{3,2,1,0:T(8,128)(2,1)S(1)}, bf16[12,8,16,256]{3,2,1,0:T(8,128)(2,1)}, u32[]{:S(2)}) copy-start(bf16[12,8,16,256]{3,2,1,0:T(8,128)(2,1)} %copy.148) | copy-start | bytes 2359300
  117.6 1.4 copy-start.3
  120.1 1.1 copy-start.5
  123.8 68.0 %copy-start.9 = (pred[224,320]{1,0:T(32,128)(4,1)S(1)}, pred[224,320]{1,0:T(32,128)(4,1)}, u32[]{:S(2)}) copy-start(pred[224,320]{1,0:T(32,128)(4,1)} %copy-done.8) | copy-start | bytes 215044

commit v11 on v5

--- a/solution.py
+++ b/solution.py
@@ -79,7 +79,6 @@
     activated = pre_gate * sigmoid_gate
     hidden = (activated * pre_up).astype(jnp.bfloat16)
     outputs = jnp.dot(hidden, down_shard, preferred_element_type=jnp.float32).astype(jnp.bfloat16)
-    outputs = lax.optimization_barrier(outputs)
     inner = jnp.sum(
         rows_cot.astype(jnp.float32) * outputs.astype(jnp.float32), axis=1
     ).astype(jnp.bfloat16)

time: 193 us -> 193 us (level)
  no operation moved by 1% of the time
where the time goes in v11:
time: 193 us
  blocking collectives  162 us (84%)
  local copies, waits for them, and re-layouts  8.35 us (4%)
  other arithmetic  6.52 us (3%)
  matrix products  6.1 us (3%)
  starting transfers between devices  5.77 us (3%)
  waiting for transfers between devices  3.35 us (2%)
    all_to_all x1, blocking collectives, shards(): lax.all_to_all(payload, 'expert', split_axis=0, concat_axis=0, tiled=True)  69.6 us
    all_to_all x1, blocking collectives, shards(): lax.all_to_all(back_send, 'expert', split_axis=0, concat_axis=0, tiled=True)  33.8 us
    all_to_all x1, blocking collectives, shards(): lax.all_to_all(ex_send, ('l', 'sy', 'sx', 'c'), split_axis=0, concat_axis...  32.1 us
    all_to_all x1, blocking collectives, shards(): lax.all_to_all(spread, ('sy', 'sx'), split_axis=0, concat_axis=0, tiled=T...  26 us
    ppermute x1, starting transfers between devices, shards(): other_core = lax.ppermute(same_core, 'c', perm=[(0, 1), (1, 0)])  5.77 us
    unnamed x12, local copies, waits for them, and re-layouts  3.88 us
  transfers between devices with their start and end apart: 1, of which 1 were waited for; matrix products, arithmetic and copies ran while one was open for 0% of the time, Pallas kernels for 0%

profile of v11, /device:TPU:1, one launch (start us, length us, event | category | flops | bytes accessed | tf_op | source)
XLA Modules:
  0.0 192.7 jit_solution(8339608017070486783)
XLA Ops:
  0.6 0.8 copy.142
  1.7 0.9 reduce-window.16
  2.9 0.9 reduce-window.14
  4.4 0.8 copy.151
  6.2 0.8 constant_dynamic-slice_fusion
  6.9 0.3 convolution_convert_fusion.1
  7.5 69.6 %all_to_all.20 = bf16[32,8,512]{2,1,0:T(8,128)(2,1)S(1)} all-to-all(bf16[32,8,512]{2,1,0:T(8,128)(2,1)S(1)} %fusion.22), channel_id=1, replica_groups=mesh['l'=2,'sy'=2,'sx'=4,'c'=2,'expert'=32] {'expert'}, dimensions={0} | all-to-all | bytes 524288 | tf_op jit(solution)/shard_map/all_to_all | solution.py:58
  77.3 26.0 %all_to_all.21 = bf16[8,224,512]{2,1,0:T(8,128)(2,1)S(1)} all-to-all(bf16[8,224,512]{2,1,0:T(8,128)(2,1)S(1)} %broadcast_in_dim.12), channel_id=1, replica_groups=mesh['l'=2,'sy'=2,'sx'=4,'c'=2,'expert'=32] {'sy','sx'}, dimensions={0} | all-to-all | bytes 3670016 | tf_op jit(solution)/shard_map/all_to_all | solution.py:64
  103.4 5.8 %collective-permute-start = (bf16[8,224,512]{2,1,0:T(8,128)(2,1)S(1)}, bf16[8,224,512]{2,1,0:T(8,128)(2,1)}, u32[]{:S(2)}, u32[]{:S(2)}) collective-permute-start(bf16[8,224,512]{2,1,0:T(8,128)(2,1)S(1)} %all_to_all.21), channel_id=1, source_target_pairs={{0,32},{32,0},{1,33},{33,1},{2,34},{34,2},{3,35},{35,3},{4,36},{36... | collective-permute-start | bytes 5505032 | tf_op jit(solution)/shard_map/ppermute | solution.py:65
  109.3 3.4 %collective-permute-done = bf16[8,224,512]{2,1,0:T(8,128)(2,1)} collective-permute-done((bf16[8,224,512]{2,1,0:T(8,128)(2,1)S(1)}, bf16[8,224,512]{2,1,0:T(8,128)(2,1)}, u32[]{:S(2)}, u32[]{:S(2)}) %collective-permute-start) | collective-permute-done | bytes 1835040 | tf_op jit(solution)/shard_map/ppermute | solution.py:65
  112.7 3.2 %fusion.4 = bf16[8,2,224,512]{3,2,0,1:T(8,128)(2,1)S(1)} fusion(s32[]{:T(128)S(6)} %select_n.90, bf16[8,1,224,512]{3,2,0,1:T(8,128)(2,1)S(1)} %bitcast.101, bf16[8,1,224,512]{3,2,0,1:T(8,128)(2,1)} %bitcast.4), kind=kLoop, calls=%fused_computation.10 | loop fusion | flops 3670016 | bytes 7340036 | tf_op jit(solution)/shard_map/stack | solution.py:66
  115.9 0.3 copy.153
  116.7 0.7 fusion.9
  117.5 0.4 copy-done.1
  117.9 0.7 fusion.12
  118.8 0.9 copy-done.2
  119.7 0.7 convolution_multiply_fusion
  120.4 0.8 fusion.5
  121.2 0.7 fusion.7
  121.9 0.7 fusion.6
  123.1 32.1 %all_to_all.22 = bf16[32,240,128]{2,1,0:T(8,128)(2,1)S(1)} all-to-all(bf16[32,240,128]{2,1,0:T(8,128)(2,1)S(1)} %pad_maximum_fusion), channel_id=1, replica_groups=mesh['l'=2,'sy'=2,'sx'=4,'c'=2,'expert'=32] {'l','sy','sx','c'}, dimensions={0} | all-to-all | bytes 3932160 | tf_op jit(solution)/shard_map/all_to_all | solution.py:105
  156.0 33.8 %all_to_all.23 = bf16[32,2,8,128]{3,1,2,0:T(2,128)(2,1)S(1)} all-to-all(bf16[32,2,8,128]{3,1,2,0:T(2,128)(2,1)S(1)} %fusion.25), channel_id=1, replica_groups=mesh['l'=2,'sy'=2,'sx'=4,'c'=2,'expert'=32] {'expert'}, dimensions={0} | all-to-all | bytes 262144 | tf_op jit(solution)/shard_map/all_to_all | solution.py:117
  191.1 0.8 convolution_convert_fusion.2
  192.0 0.7 copy.164
  (69 shorter events, 5.9 us)
Async XLA Ops:
  0.6 116.1 %copy-start = (bf16[1,96,4096]{2,1,0:T(8,128)(2,1)S(1)}, bf16[1,96,4096]{2,1,0:T(8,128)(2,1)}, u32[]{:S(2)}) copy-start(bf16[1,96,4096]{2,1,0:T(8,128)(2,1)} %param.11) | copy-start | bytes 2359300
  103.4 9.3 %collective-permute-start = (bf16[8,224,512]{2,1,0:T(8,128)(2,1)S(1)}, bf16[8,224,512]{2,1,0:T(8,128)(2,1)}, u32[]{:S(2)}, u32[]{:S(2)}) collective-permute-start(bf16[8,224,512]{2,1,0:T(8,128)(2,1)S(1)} %all_to_all.21), channel_id=1, source_target_pairs={{0,32},{32,0},{1,33},{33,1},{2,34},{34,2},{3,35},{35,3},{4,36},{36... | collective-permute-start | bytes 5505032 | tf_op jit(solution)/shard_map/ppermute | solution.py:65
  116.7 1.1 copy-start.1
  118.6 1.1 copy-start.2
